TPU v7x, 512 devices: a whole 4x4x16 slice. The times are simulated.
512 devices in a mesh: lat: 32 (over z_lo, x), lon: 16 (over y, z_hi, core).
Axes of the slice: x: 4, y: 4, z: 16 (z_hi: 2, z_lo: 8; z = z_hi * 8 + z_lo), core: 2. Of those that a mesh axis runs over, the one named last changes fastest.
Arguments:
- cotangent: bfloat16 [512, 1440, 256], P('lat', 'lon'), may hold values from -6 to 6
- legendre: bfloat16 [512, 384, 192], P('lat', 'lon'), may hold values from -0.25 to 0.25
- spectral_weight: bfloat16 [256, 256], replicated, may hold values from -0.375 to 0.375
- skip_weight: bfloat16 [256, 256], replicated, may hold values from -0.375 to 0.375
Outputs:
- grad_input: bfloat16 [512, 1440, 256], P('lat', 'lon')
All inputs are finite; a program needn't handle non-finite values.
Results may differ from a plain program's by a relative error of at most 0.015.
Values may be sent and summed in bfloat16 or wider, within the bound.
No kernel may reach another device: no remote copies, remote signals or barrier semaphores. Data moves between devices by JAX's collectives and lax.ppermute only.
A program may use at most 64 MiB of HBM per device.

v0:
```python
import math

import numpy as np

import jax
import jax.numpy as jnp
from jax import lax
from jax.sharding import PartitionSpec as P


def fourier_table(count_lon, count_wave):
    longitude = lax.broadcasted_iota(jnp.int32, (count_lon, 2 * count_wave), 0)
    column = lax.broadcasted_iota(jnp.int32, (count_lon, 2 * count_wave), 1)
    phases = (longitude * (column // 2) + (count_lon // 4) * (column % 2)) % count_lon
    angles = phases.astype(jnp.float32) * (2.0 * math.pi / count_lon)
    table = math.sqrt(2.0 / count_lon) * jnp.cos(angles)
    high = lax.reduce_precision(table, exponent_bits=8, mantissa_bits=7)
    return lax.optimization_barrier((high.astype(jnp.bfloat16), (table - high).astype(jnp.bfloat16)))


def split_dot(table_hi, table_lo, values, dims):
    dot = lambda t: lax.dot_general(t, values, dims, preferred_element_type=jnp.float32)
    return dot(table_hi) + dot(table_lo)


def unit_slots(lat_count, units_per_dev):
    first = [(units_per_dev * t) // 4 for t in range(lat_count)]
    last = [(units_per_dev * t + units_per_dev - 1) // 4 for t in range(lat_count)]
    return np.stack([np.array(first), np.array(last)], axis=1)


def shards(cotangent, legendre, spectral_weight, skip_weight):
    lat_rows, lon_dev, width = cotangent.shape
    lat_count = lax.axis_size("lat")
    lon_count = lax.axis_size("lon")
    count_lon = lon_dev * lon_count
    wave_dev = legendre.shape[1]
    half_deg = legendre.shape[2]
    all_rows = lat_rows * lat_count
    half_rows = all_rows // 2
    table_hi, table_lo = fourier_table(count_lon, wave_dev * lon_count)

    row_grid = lax.all_to_all(cotangent, "lon", 0, 0, tiled=True).reshape(count_lon, width)
    spectra = split_dot(table_hi, table_lo, row_grid, (((0,), (0,)), ((), ())))
    coeffs = lax.all_to_all(
        spectra.astype(jnp.bfloat16).reshape(lon_count, 2 * wave_dev, width), "lon", 0, 0, tiled=True
    )
    units_total = wave_dev * 4
    units_per_dev = units_total // lat_count
    unit_width = width // 2
    unit_send = coeffs.reshape(lat_rows, lat_count, units_per_dev * unit_width)
    slots = unit_slots(lat_count, units_per_dev)
    basis_send = jnp.take(legendre, jnp.asarray(slots.reshape(-1)), axis=1).reshape(
        lat_rows, lat_count, 2 * half_deg
    )
    payload = jnp.concatenate([unit_send, basis_send], axis=-1).transpose(1, 0, 2)
    arrived = lax.all_to_all(payload, "lat", 0, 0, tiled=True).reshape(all_rows, -1)
    gathered = arrived[:, : units_per_dev * unit_width].reshape(all_rows, units_per_dev, unit_width)
    basis_recv = arrived[:, units_per_dev * unit_width :].reshape(all_rows, 2, half_deg)

    band = lax.axis_index("lat")
    unit_ids = units_per_dev * band + jnp.arange(units_per_dev)
    local_wave = unit_ids // 4
    use_last = (local_wave - (units_per_dev * band) // 4) > 0
    basis = jnp.where(
        use_last[None, :, None], basis_recv[:, 1:2, :], basis_recv[:, 0:1, :]
    )
    wavenum = lax.axis_index("lon") * wave_dev + local_wave
    degree = 2 * jnp.arange(half_deg)
    parity = wavenum % 2
    mask_even = degree[None, :] + parity[:, None] >= wavenum[:, None]
    mask_odd = degree[None, :] + 1 - parity[:, None] >= wavenum[:, None]
    north_basis = jnp.where(mask_even[None], basis[:half_rows], jnp.zeros_like(basis[:half_rows]))
    south_basis = jnp.where(mask_odd[None], basis[half_rows:], jnp.zeros_like(basis[half_rows:]))

    north_wide = gathered[:half_rows].astype(jnp.float32)
    south_wide = gathered[half_rows:].astype(jnp.float32)
    comb_even = (north_wide + south_wide).astype(jnp.bfloat16)
    comb_odd = (north_wide - south_wide).astype(jnp.bfloat16)
    deg_even = jnp.einsum(
        "nuk,nuc->ukc", north_basis, comb_even, preferred_element_type=jnp.float32
    ).astype(jnp.bfloat16)
    deg_odd = jnp.einsum(
        "nuk,nuc->ukc", south_basis, comb_odd, preferred_element_type=jnp.float32
    ).astype(jnp.bfloat16)
    proj_even = jnp.einsum(
        "nuk,ukc->nuc", north_basis, deg_even, preferred_element_type=jnp.float32
    ).astype(jnp.bfloat16).astype(jnp.float32)
    proj_odd = jnp.einsum(
        "nuk,ukc->nuc", south_basis, deg_odd, preferred_element_type=jnp.float32
    ).astype(jnp.bfloat16).astype(jnp.float32)
    grad_units = jnp.concatenate([proj_even + proj_odd, proj_even - proj_odd], 0).astype(
        jnp.bfloat16
    )
    returned = lax.all_to_all(
        grad_units.reshape(lat_count, lat_rows, units_per_dev * unit_width), "lat", 0, 0, tiled=True
    ).transpose(1, 0, 2).reshape(lat_rows, 2 * wave_dev, width)

    row_coeffs = lax.all_to_all(returned, "lon", 0, 0, tiled=True).reshape(2 * wave_dev * lon_count, width)
    grid_part = split_dot(table_hi, table_lo, row_coeffs, (((1,), (0,)), ((), ())))
    spatial = lax.all_to_all(
        grid_part.astype(jnp.bfloat16).reshape(lon_count, lon_dev, width), "lon", 0, 0, tiled=True
    )
    stacked_in = jnp.concatenate([spatial, cotangent], axis=-1).reshape(-1, 2 * width)
    stacked_w = jnp.concatenate([spectral_weight, skip_weight], axis=1)
    out = jnp.dot(stacked_in, stacked_w.T, preferred_element_type=jnp.float32)
    return out.astype(jnp.bfloat16).reshape(cotangent.shape)


def solution(mesh):
    return jax.shard_map(
        shards,
        mesh=mesh,
        in_specs=(P("lat", "lon", None), P("lat", "lon", None), P(), P()),
        out_specs=P("lat", "lon", None),
        check_vma=False,
    )
```

profile of v0, /device:TPU:32, one launch (start us, length us, event | category | flops | bytes accessed | tf_op | source)
XLA Modules:
  0.0 269.5 jit_solution(16182964212515341369)
XLA Ops:
  0.0 2.3 copy.27
  2.3 16.9 %all-to-all-start = ((bf16[16,90,256]{2,1,0:T(8,128)(2,1)}), bf16[16,90,256]{2,1,0:T(8,128)(2,1)S(1)}, u32[]{:S(2)}, u32[]{:S(2)}) async-start(bf16[16,90,256]{2,1,0:T(8,128)(2,1)} %copy.27), calls=%async_computation | async-start | bytes 1572864 | tf_op jit(solution)/shard_map/all_to_all | solution.py:43
  19.2 19.0 %fusion = (bf16[1440,768]{1,0:T(8,128)(2,1)S(1)}, bf16[1440,768]{1,0:T(8,128)(2,1)}) fusion(s32[768]{0:T(1024)S(1)} %get-tuple-element.22, s32[768]{0:T(1024)S(1)} %get-tuple-element.23, pred[768]{0:T(1024)(128)(4,1)S(1)} %get-tuple-element.25, s32[768]{0:T(1024)S(1)} %get-tuple-element.21, s32[768]{0:T(1024)S(1)} %get-tuple-element.24, ...), kind=kLoop, calls=%fused_computation.4 | loop fusion | flops 19906560 | bytes 4437504 | tf_op jit(solution)/shard_map/convert_element_type | solution.py:18
  38.2 28.8 %all-to-all-done = bf16[16,90,256]{2,1,0:T(8,128)(2,1)S(1)} async-done(((bf16[16,90,256]{2,1,0:T(8,128)(2,1)}), bf16[16,90,256]{2,1,0:T(8,128)(2,1)S(1)}, u32[]{:S(2)}, u32[]{:S(2)}) %all-to-all-start) | async-done | bytes 737312 | tf_op jit(solution)/shard_map/all_to_all | solution.py:43
  67.0 1.1 reshape.195
  68.0 2.7 fusion.41
  70.7 1.6 fusion.9
  72.3 3.6 %all-to-all-start.1 = ((bf16[16,48,256]{2,1,0:T(8,128)(2,1)}), bf16[16,48,256]{2,1,0:T(8,128)(2,1)S(1)}, u32[]{:S(2)}, u32[]{:S(2)}) async-start(bf16[16,48,256]{2,1,0:T(8,128)(2,1)} %bitcast), calls=%async_computation.1 | async-start | bytes 786432 | tf_op jit(solution)/shard_map/all_to_all | solution.py:45
  75.9 2.1 gather_fusion
  78.0 1.1 gather.7
  79.1 14.9 %all-to-all-done.1 = bf16[16,48,256]{2,1,0:T(8,128)(2,1)S(1)} async-done(((bf16[16,48,256]{2,1,0:T(8,128)(2,1)}), bf16[16,48,256]{2,1,0:T(8,128)(2,1)S(1)}, u32[]{:S(2)}, u32[]{:S(2)}) %all-to-all-start.1) | async-done | bytes 393248 | tf_op jit(solution)/shard_map/all_to_all | solution.py:45
  94.2 1.1 maximum_bitcast_fusion
  95.3 1.3 copy.28
  96.6 9.9 %all-to-all-start.2 = ((bf16[32,16,768]{2,1,0:T(8,128)(2,1)}), bf16[32,16,768]{2,1,0:T(8,128)(2,1)S(1)}, u32[]{:S(2)}, u32[]{:S(2)}) async-start(bf16[32,16,768]{2,1,0:T(8,128)(2,1)} %copy.28), calls=%async_computation.2 | async-start | bytes 1572864 | tf_op jit(solution)/shard_map/all_to_all | solution.py:57
  106.7 40.1 %all-to-all-done.2 = bf16[32,16,768]{2,1,0:T(8,128)(2,1)S(1)} async-done(((bf16[32,16,768]{2,1,0:T(8,128)(2,1)}), bf16[32,16,768]{2,1,0:T(8,128)(2,1)S(1)}, u32[]{:S(2)}, u32[]{:S(2)}) %all-to-all-start.2) | async-done | bytes 786464 | tf_op jit(solution)/shard_map/all_to_all | solution.py:57
  146.8 0.8 slice.35
  147.6 0.8 fusion.13
  148.4 1.2 copy.29
  149.6 1.1 copy.32
  150.8 0.9 broadcast_select_fusion
  151.7 1.6 fusion.10
  153.3 1.6 fusion.21
  155.3 0.3 convert_element_type.83
  155.7 29.6 %all_to_all.30 = bf16[32,16,384]{2,1,0:T(8,128)(2,1)S(1)} all-to-all(bf16[32,16,384]{2,1,0:T(8,128)(2,1)S(1)} %convert_element_type.83), channel_id=1, replica_groups=mesh['lat'=32,'lon'=16] {'lat'}, dimensions={0} | all-to-all | bytes 786432 | tf_op jit(solution)/shard_map/all_to_all | solution.py:95
  185.6 33.4 %all_to_all.31 = bf16[16,48,256]{2,1,0:T(8,128)(2,1)S(1)} all-to-all(bf16[16,48,256]{2,1,0:T(8,128)(2,1)S(1)} %reshape.200), channel_id=1, replica_groups=mesh['lat'=32,'lon'=16] {'lon'}, dimensions={0} | all-to-all | bytes 786432 | tf_op jit(solution)/shard_map/all_to_all | solution.py:99
  219.0 2.4 fusion.42
  221.4 0.8 fusion.8
  222.4 41.0 %all_to_all.32 = bf16[16,90,256]{2,1,0:T(8,128)(2,1)S(1)} all-to-all(bf16[16,90,256]{2,1,0:T(8,128)(2,1)S(1)} %reshape.202), channel_id=1, replica_groups=mesh['lat'=32,'lon'=16] {'lon'}, dimensions={0} | all-to-all | bytes 1474560 | tf_op jit(solution)/shard_map/all_to_all | solution.py:101
  263.4 1.3 pad_maximum_fusion
  264.7 1.4 reshape.203
  266.0 1.9 convolution_convert_fusion
  268.2 1.3 copy.37
  (27 shorter events, 1.6 us)
Async XLA Ops:
  0.0 75.9 %copy-start = (bf16[16,24,192]{2,1,0:T(8,128)(2,1)S(1)}, bf16[16,24,192]{2,1,0:T(8,128)(2,1)}, u32[]{:S(2)}) copy-start(bf16[16,24,192]{2,1,0:T(8,128)(2,1)} %param.6) | copy-start | bytes 442372
  2.3 64.7 %all-to-all-start = ((bf16[16,90,256]{2,1,0:T(8,128)(2,1)}), bf16[16,90,256]{2,1,0:T(8,128)(2,1)S(1)}, u32[]{:S(2)}, u32[]{:S(2)}) async-start(bf16[16,90,256]{2,1,0:T(8,128)(2,1)} %copy.27), calls=%async_computation | async-start | bytes 1572864 | tf_op jit(solution)/shard_map/all_to_all | solution.py:43
  68.0 2.7 copy-start.1
  70.7 5.2 %copy-start.2 = (s32[64]{0:T(128)S(1)}, s32[64]{0:T(128)}, u32[]{:S(2)}) copy-start(s32[64]{0:T(128)} %constant.119) | copy-start | bytes 772
  72.3 21.7 %all-to-all-start.1 = ((bf16[16,48,256]{2,1,0:T(8,128)(2,1)}), bf16[16,48,256]{2,1,0:T(8,128)(2,1)S(1)}, u32[]{:S(2)}, u32[]{:S(2)}) async-start(bf16[16,48,256]{2,1,0:T(8,128)(2,1)} %bitcast), calls=%async_computation.1 | async-start | bytes 786432 | tf_op jit(solution)/shard_map/all_to_all | solution.py:45
  96.6 50.2 %all-to-all-start.2 = ((bf16[32,16,768]{2,1,0:T(8,128)(2,1)}), bf16[32,16,768]{2,1,0:T(8,128)(2,1)S(1)}, u32[]{:S(2)}, u32[]{:S(2)}) async-start(bf16[32,16,768]{2,1,0:T(8,128)(2,1)} %copy.28), calls=%async_computation.2 | async-start | bytes 1572864 | tf_op jit(solution)/shard_map/all_to_all | solution.py:57
  264.7 1.4 copy-start.3
  264.7 1.4 copy-start.4
where the time goes:
time: 270 us; the launch traced here: 269 us
  blocking collectives  104 us (39%)
  waiting for transfers between devices  83.7 us (31%)
  starting transfers between devices  30.4 us (11%)
  other arithmetic  23.2 us (9%)
  local copies, waits for them, and re-layouts  15.3 us (6%)
  matrix products  12.6 us (5%)
    all_to_all x1, blocking collectives, shards(): lax.all_to_all(grid_part.astype(jnp.bfloat16).reshape(lon_count, lon_dev,...  41 us
    all_to_all x1, waiting for transfers between devices, shards(): lax.all_to_all(payload, 'lat', 0, 0, tiled=True).reshape(all_rows, -1)  40.1 us
    all_to_all x1, blocking collectives, shards(): lax.all_to_all(returned, 'lon', 0, 0, tiled=True)  33.4 us
    all_to_all x1, blocking collectives, shards(): lax.all_to_all(grad_units.reshape(lat_count, lat_rows, units_per_dev * un...  29.6 us
    all_to_all x1, waiting for transfers between devices, shards(): lax.all_to_all(cotangent, 'lon', 0, 0, tiled=True).reshape(count_lon, width)  28.8 us
    convert_element_type x1, other arithmetic, fourier_table(): (table - high).astype(jnp.bfloat16)  19 us
    all_to_all x1, starting transfers between devices, shards(): lax.all_to_all(cotangent, 'lon', 0, 0, tiled=True).reshape(count_lon, width)  16.9 us
    all_to_all x1, waiting for transfers between devices, shards(): lax.all_to_all(spectra.astype(jnp.bfloat16).reshape(lon_count, 2 * wave_d...  14.9 us
  transfers between devices with their start and end apart: 3, of which 3 were waited for; matrix products, arithmetic and copies ran while one was open for 8% of the time, Pallas kernels for 0%

commit v1 on v0

--- a/solution.py
+++ b/solution.py
@@ -39,6 +39,7 @@
     all_rows = lat_rows * lat_count
     half_rows = all_rows // 2
     table_hi, table_lo = fourier_table(count_lon, wave_dev * lon_count)
+    skip_term = jnp.einsum("rlc,dc->rld", cotangent, skip_weight, preferred_element_type=jnp.float32)
 
     row_grid = lax.all_to_all(cotangent, "lon", 0, 0, tiled=True).reshape(count_lon, width)
     spectra = split_dot(table_hi, table_lo, row_grid, (((0,), (0,)), ((), ())))
@@ -48,12 +49,12 @@
     units_total = wave_dev * 4
     units_per_dev = units_total // lat_count
     unit_width = width // 2
-    unit_send = coeffs.reshape(lat_rows, lat_count, units_per_dev * unit_width)
+    unit_send = coeffs.reshape(lat_rows, lat_count, units_per_dev * unit_width).transpose(1, 0, 2)
     slots = unit_slots(lat_count, units_per_dev)
-    basis_send = jnp.take(legendre, jnp.asarray(slots.reshape(-1)), axis=1).reshape(
-        lat_rows, lat_count, 2 * half_deg
+    basis_send = jnp.stack(
+        [jnp.concatenate([legendre[:, a], legendre[:, b]], axis=-1) for a, b in slots.tolist()]
     )
-    payload = jnp.concatenate([unit_send, basis_send], axis=-1).transpose(1, 0, 2)
+    payload = jnp.concatenate([unit_send, basis_send], axis=-1)
     arrived = lax.all_to_all(payload, "lat", 0, 0, tiled=True).reshape(all_rows, -1)
     gathered = arrived[:, : units_per_dev * unit_width].reshape(all_rows, units_per_dev, unit_width)
     basis_recv = arrived[:, units_per_dev * unit_width :].reshape(all_rows, 2, half_deg)
@@ -101,10 +102,8 @@
     spatial = lax.all_to_all(
         grid_part.astype(jnp.bfloat16).reshape(lon_count, lon_dev, width), "lon", 0, 0, tiled=True
     )
-    stacked_in = jnp.concatenate([spatial, cotangent], axis=-1).reshape(-1, 2 * width)
-    stacked_w = jnp.concatenate([spectral_weight, skip_weight], axis=1)
-    out = jnp.dot(stacked_in, stacked_w.T, preferred_element_type=jnp.float32)
-    return out.astype(jnp.bfloat16).reshape(cotangent.shape)
+    mixed = jnp.einsum("rlc,dc->rld", spatial, spectral_weight, preferred_element_type=jnp.float32)
+    return (mixed + skip_term).astype(jnp.bfloat16)
 
 
 def solution(mesh):

time: 270 us -> 271 us (level)
  local copies, waits for them, and re-layouts: 15.3 us -> 25.3 us
  waiting for transfers between devices: 83.7 us -> 77.8 us
    another operation x0 -> x33, local copies, waits for them, and re-layouts: none -> 14.4 us  [shards(): jnp.stack([jnp.concatenate([legendre[:, a], legendre[:, b]], axis=-1) for...]
    all_to_all x1, waiting for transfers between devices: 28.8 us -> 18 us  [shards(): lax.all_to_all(cotangent, 'lon', 0, 0, tiled=True).reshape(count_lon, width)]
    all_to_all x1, waiting for transfers between devices: 14.9 us -> 19.7 us  [shards(): lax.all_to_all(spectra.astype(jnp.bfloat16).reshape(lon_count, 2 * wave_d...]
    gather x2 -> x0, local copies, waits for them, and re-layouts: 3.2 us -> none  [shards(): jnp.take(legendre, jnp.asarray(slots.reshape(-1)), axis=1)]
    reshape x4 -> x1, local copies, waits for them, and re-layouts: 3.06 us -> 0.24 us  [shards(): coeffs.reshape(lat_rows, lat_count, units_per_dev * unit_width)]
  transfers between devices with their start and end apart: 3 -> 3, of which waited for: 3 -> 3; matrix products, arithmetic and copies ran while one was open for 8% -> 13% of each run, Pallas kernels for 0% -> 0%
where the time goes in v1:
time: 271 us; the launch traced here: 270 us
  blocking collectives  104 us (38%)
  waiting for transfers between devices  77.8 us (29%)
  starting transfers between devices  28.8 us (11%)
  local copies, waits for them, and re-layouts  25.3 us (9%)
  other arithmetic  21.7 us (8%)
  matrix products  11.6 us (4%)
    all_to_all x1, blocking collectives, shards(): lax.all_to_all(grid_part.astype(jnp.bfloat16).reshape(lon_count, lon_dev,...  41.1 us
    all_to_all x1, waiting for transfers between devices, shards(): lax.all_to_all(payload, 'lat', 0, 0, tiled=True).reshape(all_rows, -1)  40.1 us
    all_to_all x1, blocking collectives, shards(): lax.all_to_all(returned, 'lon', 0, 0, tiled=True)  33.4 us
    all_to_all x1, blocking collectives, shards(): lax.all_to_all(grad_units.reshape(lat_count, lat_rows, units_per_dev * un...  29.6 us
    all_to_all x1, waiting for transfers between devices, shards(): lax.all_to_all(spectra.astype(jnp.bfloat16).reshape(lon_count, 2 * wave_d...  19.7 us
    convert_element_type x1, other arithmetic, fourier_table(): (table - high).astype(jnp.bfloat16)  19 us
    all_to_all x1, waiting for transfers between devices, shards(): lax.all_to_all(cotangent, 'lon', 0, 0, tiled=True).reshape(count_lon, width)  18 us
    all_to_all x1, starting transfers between devices, shards(): lax.all_to_all(cotangent, 'lon', 0, 0, tiled=True).reshape(count_lon, width)  16.9 us
  transfers between devices with their start and end apart: 3, of which 3 were waited for; matrix products, arithmetic and copies ran while one was open for 13% of the time, Pallas kernels for 0%

profile of v1, /device:TPU:32, one launch (start us, length us, event | category | flops | bytes accessed | tf_op | source)
XLA Modules:
  0.0 269.8 jit_solution(5631524831436281270)
XLA Ops:
  0.0 2.3 copy.329
  2.3 16.9 %all-to-all-start = ((bf16[16,90,256]{2,1,0:T(8,128)(2,1)}), bf16[16,90,256]{2,1,0:T(8,128)(2,1)S(1)}, u32[]{:S(2)}, u32[]{:S(2)}) async-start(bf16[16,90,256]{2,1,0:T(8,128)(2,1)} %copy.329), calls=%async_computation | async-start | bytes 1572864 | tf_op jit(solution)/shard_map/all_to_all | solution.py:44
  19.2 1.0 fusion.73
  20.3 0.6 copy.363
  22.3 0.6 copy.366
  26.1 0.6 copy.372
  27.4 0.6 copy.374
  28.6 0.6 copy.376
  29.9 19.0 %fusion = (bf16[1440,768]{1,0:T(8,128)(2,1)S(1)}, bf16[1440,768]{1,0:T(8,128)(2,1)}) fusion(s32[768]{0:T(1024)S(1)} %get-tuple-element.78, s32[768]{0:T(1024)S(1)} %get-tuple-element.79, pred[768]{0:T(1024)(128)(4,1)S(1)} %get-tuple-element.81, s32[768]{0:T(1024)S(1)} %get-tuple-element.77, s32[768]{0:T(1024)S(1)} %get-tuple-element.80, ...), kind=kLoop, calls=%fused_computation.3 | loop fusion | flops 19906560 | bytes 4437504 | tf_op jit(solution)/shard_map/convert_element_type | solution.py:18
  48.9 18.0 %all-to-all-done = bf16[16,90,256]{2,1,0:T(8,128)(2,1)S(1)} async-done(((bf16[16,90,256]{2,1,0:T(8,128)(2,1)}), bf16[16,90,256]{2,1,0:T(8,128)(2,1)S(1)}, u32[]{:S(2)}, u32[]{:S(2)}) %all-to-all-start) | async-done | bytes 737312 | tf_op jit(solution)/shard_map/all_to_all | solution.py:44
  66.9 1.1 reshape.178
  68.0 2.7 fusion.75
  70.7 1.6 fusion.9
  72.3 3.6 %all-to-all-start.1 = ((bf16[16,48,256]{2,1,0:T(8,128)(2,1)}), bf16[16,48,256]{2,1,0:T(8,128)(2,1)S(1)}, u32[]{:S(2)}, u32[]{:S(2)}) async-start(bf16[16,48,256]{2,1,0:T(8,128)(2,1)} %bitcast.154), calls=%async_computation.1 | async-start | bytes 786432 | tf_op jit(solution)/shard_map/all_to_all | solution.py:46
  77.3 0.6 copy.357
  77.9 3.6 %stack.131 = bf16[32,16,384]{2,0,1:T(8,128)(2,1)S(1)} concatenate(bf16[1,16,384]{2,0,1:T(2,128)(2,1)S(1)} %copy.354, bf16[1,16,384]{2,0,1:T(2,128)(2,1)S(1)} %copy.355, bf16[1,16,384]{2,0,1:T(2,128)(2,1)} %copy.356, bf16[1,16,384]{2,0,1:T(2,128)(2,1)} %copy.357, bf16[1,16,384]{2,0,1:T(2,128)(2,1)S(1)} %copy.358, bf16[1,16,384]{2,0,1:T(2,128)(2,1)S(1)} %copy.359, ...), dimensions={0} | concatenate | bytes 786432 | tf_op jit(solution)/shard_map/stack | solution.py:54
  81.6 19.7 %all-to-all-done.1 = bf16[16,48,256]{2,1,0:T(8,128)(2,1)S(1)} async-done(((bf16[16,48,256]{2,1,0:T(8,128)(2,1)}), bf16[16,48,256]{2,1,0:T(8,128)(2,1)S(1)}, u32[]{:S(2)}, u32[]{:S(2)}) %all-to-all-start.1) | async-done | bytes 393248 | tf_op jit(solution)/shard_map/all_to_all | solution.py:46
  101.6 1.3 copy.386
  102.9 8.4 %all-to-all-start.2 = ((bf16[32,16,768]{2,1,0:T(8,128)(2,1)}), bf16[32,16,768]{2,1,0:T(8,128)(2,1)S(1)}, u32[]{:S(2)}, u32[]{:S(2)}) async-start(bf16[32,16,768]{2,1,0:T(8,128)(2,1)} %copy.386), calls=%async_computation.2 | async-start | bytes 1572864 | tf_op jit(solution)/shard_map/all_to_all | solution.py:58
  111.5 40.1 %all-to-all-done.2 = bf16[32,16,768]{2,1,0:T(8,128)(2,1)S(1)} async-done(((bf16[32,16,768]{2,1,0:T(8,128)(2,1)}), bf16[32,16,768]{2,1,0:T(8,128)(2,1)S(1)}, u32[]{:S(2)}, u32[]{:S(2)}) %all-to-all-start.2) | async-done | bytes 786464 | tf_op jit(solution)/shard_map/all_to_all | solution.py:58
  151.6 0.8 fusion.13
  152.7 1.1 copy.390
  153.7 1.1 copy.388
  154.8 0.9 broadcast_select_fusion
  155.7 1.6 fusion.10
  157.4 1.6 fusion.18
  159.7 29.6 %all_to_all.30 = bf16[32,16,384]{2,1,0:T(8,128)(2,1)S(1)} all-to-all(bf16[32,16,384]{2,1,0:T(8,128)(2,1)S(1)} %convert_element_type.83), channel_id=1, replica_groups=mesh['lat'=32,'lon'=16] {'lat'}, dimensions={0} | all-to-all | bytes 786432 | tf_op jit(solution)/shard_map/all_to_all | solution.py:96
  189.6 33.4 %all_to_all.31 = bf16[16,48,256]{2,1,0:T(8,128)(2,1)S(1)} all-to-all(bf16[16,48,256]{2,1,0:T(8,128)(2,1)S(1)} %reshape.183), channel_id=1, replica_groups=mesh['lat'=32,'lon'=16] {'lon'}, dimensions={0} | all-to-all | bytes 786432 | tf_op jit(solution)/shard_map/all_to_all | solution.py:100
  223.0 2.4 fusion.76
  225.4 0.8 fusion.8
  226.4 41.1 %all_to_all.32 = bf16[16,90,256]{2,1,0:T(8,128)(2,1)S(1)} all-to-all(bf16[16,90,256]{2,1,0:T(8,128)(2,1)S(1)} %reshape.185), channel_id=1, replica_groups=mesh['lat'=32,'lon'=16] {'lon'}, dimensions={0} | all-to-all | bytes 1474560 | tf_op jit(solution)/shard_map/all_to_all | solution.py:102
  268.5 1.3 copy.395
  (84 shorter events, 10.7 us)
Async XLA Ops:
  0.0 267.5 %copy-start = (bf16[256,256]{1,0:T(8,128)(2,1)S(1)}, bf16[256,256]{1,0:T(8,128)(2,1)}, u32[]{:S(2)}) copy-start(bf16[256,256]{1,0:T(8,128)(2,1)} %param.6) | copy-start | bytes 393220
  0.0 19.2 %copy-start.2 = (bf16[16,24,192]{2,1,0:T(8,128)(2,1)S(1)}, bf16[16,24,192]{2,1,0:T(8,128)(2,1)}, u32[]{:S(2)}) copy-start(bf16[16,24,192]{2,1,0:T(8,128)(2,1)} %param.5) | copy-start | bytes 442372
  2.3 64.6 %all-to-all-start = ((bf16[16,90,256]{2,1,0:T(8,128)(2,1)}), bf16[16,90,256]{2,1,0:T(8,128)(2,1)S(1)}, u32[]{:S(2)}, u32[]{:S(2)}) async-start(bf16[16,90,256]{2,1,0:T(8,128)(2,1)} %copy.329), calls=%async_computation | async-start | bytes 1572864 | tf_op jit(solution)/shard_map/all_to_all | solution.py:44
  68.0 2.7 copy-start.3
  70.6 5.6 %copy-start.7 = (bf16[16,1,192]{2,1,0:T(2,128)(2,1)S(1)}, bf16[16,1,192]{2,1,0:T(2,128)(2,1)}, u32[]{:S(2)}) copy-start(bf16[16,1,192]{2,1,0:T(2,128)(2,1)} %get-tuple-element.35) | copy-start | bytes 18436
  70.7 7.3 %copy-start.5 = (bf16[1,16,384]{2,0,1:T(2,128)(2,1)S(1)}, bf16[1,16,384]{2,0,1:T(2,128)(2,1)}, u32[]{:S(2)}) copy-start(bf16[1,16,384]{2,0,1:T(2,128)(2,1)} %copy.363) | copy-start | bytes 36868
  70.7 7.3 %copy-start.6 = (bf16[1,16,384]{2,0,1:T(2,128)(2,1)S(1)}, bf16[1,16,384]{2,0,1:T(2,128)(2,1)}, u32[]{:S(2)}) copy-start(bf16[1,16,384]{2,0,1:T(2,128)(2,1)} %copy.364) | copy-start | bytes 36868
  72.3 29.0 %all-to-all-start.1 = ((bf16[16,48,256]{2,1,0:T(8,128)(2,1)}), bf16[16,48,256]{2,1,0:T(8,128)(2,1)S(1)}, u32[]{:S(2)}, u32[]{:S(2)}) async-start(bf16[16,48,256]{2,1,0:T(8,128)(2,1)} %bitcast.154), calls=%async_computation.1 | async-start | bytes 786432 | tf_op jit(solution)/shard_map/all_to_all | solution.py:46
  102.9 48.6 %all-to-all-start.2 = ((bf16[32,16,768]{2,1,0:T(8,128)(2,1)}), bf16[32,16,768]{2,1,0:T(8,128)(2,1)S(1)}, u32[]{:S(2)}, u32[]{:S(2)}) async-start(bf16[32,16,768]{2,1,0:T(8,128)(2,1)} %copy.386), calls=%async_computation.2 | async-start | bytes 1572864 | tf_op jit(solution)/shard_map/all_to_all | solution.py:58
  226.4 41.6 %copy-start.1 = (bf16[16,90,256]{2,0,1:T(8,128)(2,1)S(1)}, bf16[16,90,256]{2,0,1:T(8,128)(2,1)}, u32[]{:S(2)}) copy-start(bf16[16,90,256]{2,0,1:T(8,128)(2,1)} %param.4) | copy-start | bytes 2211844
  226.4 41.6 %copy-start.4 = (bf16[256,256]{1,0:T(8,128)(2,1)S(1)}, bf16[256,256]{1,0:T(8,128)(2,1)}, u32[]{:S(2)}) copy-start(bf16[256,256]{1,0:T(8,128)(2,1)} %param.7) | copy-start | bytes 393220

commit v2 on v1

--- a/solution.py
+++ b/solution.py
@@ -97,11 +97,28 @@
         grad_units.reshape(lat_count, lat_rows, units_per_dev * unit_width), "lat", 0, 0, tiled=True
     ).transpose(1, 0, 2).reshape(lat_rows, 2 * wave_dev, width)
 
-    row_coeffs = lax.all_to_all(returned, "lon", 0, 0, tiled=True).reshape(2 * wave_dev * lon_count, width)
-    grid_part = split_dot(table_hi, table_lo, row_coeffs, (((1,), (0,)), ((), ())))
+    halves = 2
+    group = lon_count // halves
+    pair_rows = lat_rows // group
+    own_half = (lax.axis_index("lon") // 2) % halves
+    by_pair = returned.reshape(lon_count // 4, 1, 2, pair_rows, 2 * wave_dev, width)
+    pair_send = jnp.broadcast_to(
+        by_pair, (lon_count // 4, halves, 2, pair_rows, 2 * wave_dev, width)
+    ).reshape(lon_count, pair_rows, 2 * wave_dev, width)
+    pair_coeffs = lax.all_to_all(pair_send, "lon", 0, 0, tiled=True)
+    pair_coeffs = pair_coeffs.transpose(1, 0, 2, 3).reshape(pair_rows, 2 * wave_dev * lon_count, width)
+    half_table = lambda t: lax.dynamic_index_in_dim(
+        t.reshape(lon_count // 4, halves, 2, lon_dev, -1), own_half, axis=1, keepdims=False
+    ).reshape(group * lon_dev, -1)
+    half_grid = split_dot(
+        half_table(table_hi), half_table(table_lo), pair_coeffs, (((1,), (1,)), ((), ()))
+    )
+    half_send = half_grid.astype(jnp.bfloat16).reshape(group, lon_dev, pair_rows, width).transpose(0, 2, 1, 3)
+    lon_ids = np.arange(lon_count).reshape(lon_count // 4, halves, 2)
+    half_groups = [lon_ids[:, h, :].reshape(-1).tolist() for h in range(halves)]
     spatial = lax.all_to_all(
-        grid_part.astype(jnp.bfloat16).reshape(lon_count, lon_dev, width), "lon", 0, 0, tiled=True
-    )
+        half_send, "lon", 0, 0, tiled=True, axis_index_groups=half_groups
+    ).reshape(lat_rows, lon_dev, width)
     mixed = jnp.einsum("rlc,dc->rld", spatial, spectral_weight, preferred_element_type=jnp.float32)
     return (mixed + skip_term).astype(jnp.bfloat16)
 

time: 271 us -> 264 us (0.974)
  blocking collectives: 104 us -> 44.6 us
  waiting for transfers between devices: 77.8 us -> 107 us
  local copies, waits for them, and re-layouts: 25.3 us -> 46.2 us
  starting transfers between devices: 28.8 us -> 32.5 us
    all_to_all x2 -> x1, blocking collectives: 74.5 us -> 15 us  [shards(): lax.all_to_all(half_send, 'lon', 0, 0, tiled=True, axis_index_groups=half...]
    all_to_all x0 -> x1, waiting for transfers between devices: none -> 36 us  [shards(): pair_coeffs = lax.all_to_all(pair_send, 'lon', 0, 0, tiled=True)]
    reshape x2 -> x4, local copies, waits for them, and re-layouts: 0.43 us -> 8.7 us  [the longest x2 6.29 us: shards(): t.reshape(lon_count // 4, halves, 2, lon_dev, -1)]
    another operation x33, local copies, waits for them, and re-layouts: 14.4 us -> 21.8 us  [shards(): jnp.stack([jnp.concatenate([legendre[:, a], legendre[:, b]], axis=-1) for...]
    all_to_all x1, waiting for transfers between devices: 19.7 us -> 12.7 us  [shards(): lax.all_to_all(spectra.astype(jnp.bfloat16).reshape(lon_count, 2 * wave_d...]
    all_to_all x0 -> x1, starting transfers between devices: none -> 3.79 us  [shards(): pair_coeffs = lax.all_to_all(pair_send, 'lon', 0, 0, tiled=True)]
  transfers between devices with their start and end apart: 3 -> 4, of which waited for: 3 -> 4; matrix products, arithmetic and copies ran while one was open for 13% -> 21% of each run, Pallas kernels for 0% -> 0%
where the time goes in v2:
time: 264 us; the launch traced here: 263 us
  waiting for transfers between devices  107 us (41%)
  local copies, waits for them, and re-layouts  46.2 us (18%)
  blocking collectives  44.6 us (17%)
  starting transfers between devices  32.5 us (12%)
  other arithmetic  21.6 us (8%)
  matrix products  11.2 us (4%)
    all_to_all x1, waiting for transfers between devices, shards(): lax.all_to_all(payload, 'lat', 0, 0, tiled=True).reshape(all_rows, -1)  40.1 us
    all_to_all x1, waiting for transfers between devices, shards(): pair_coeffs = lax.all_to_all(pair_send, 'lon', 0, 0, tiled=True)  36 us
    all_to_all x1, blocking collectives, shards(): lax.all_to_all(grad_units.reshape(lat_count, lat_rows, units_per_dev * un...  29.6 us
    another operation x33, local copies, waits for them, and re-layouts, shards(): jnp.stack([jnp.concatenate([legendre[:, a], legendre[:, b]], axis=-1) for...  21.8 us
    convert_element_type x1, other arithmetic, fourier_table(): (table - high).astype(jnp.bfloat16)  19 us
    all_to_all x1, waiting for transfers between devices, shards(): lax.all_to_all(cotangent, 'lon', 0, 0, tiled=True).reshape(count_lon, width)  17.9 us
    all_to_all x1, starting transfers between devices, shards(): lax.all_to_all(cotangent, 'lon', 0, 0, tiled=True).reshape(count_lon, width)  16.9 us
    all_to_all x1, blocking collectives, shards(): lax.all_to_all(half_send, 'lon', 0, 0, tiled=True, axis_index_groups=half...  15 us
  transfers between devices with their start and end apart: 4, of which 4 were waited for; matrix products, arithmetic and copies ran while one was open for 21% of the time, Pallas kernels for 0%

profile of v2, /device:TPU:32, one launch (start us, length us, event | category | flops | bytes accessed | tf_op | source)
XLA Modules:
  0.0 263.4 jit_solution(16156228070224525886)
XLA Ops:
  0.0 2.3 copy.345
  2.3 16.9 %all-to-all-start = ((bf16[16,90,256]{2,1,0:T(8,128)(2,1)}), bf16[16,90,256]{2,1,0:T(8,128)(2,1)S(1)}, u32[]{:S(2)}, u32[]{:S(2)}) async-start(bf16[16,90,256]{2,1,0:T(8,128)(2,1)} %copy.345), calls=%async_computation | async-start | bytes 1572864 | tf_op jit(solution)/shard_map/all_to_all | solution.py:44
  19.3 1.0 fusion.72
  30.1 19.0 %fusion = (bf16[1440,768]{1,0:T(8,128)(2,1)S(1)}, bf16[1440,768]{1,0:T(8,128)(2,1)}) fusion(s32[768]{0:T(1024)S(1)} %get-tuple-element.78, s32[768]{0:T(1024)S(1)} %get-tuple-element.79, pred[768]{0:T(1024)(128)(4,1)S(1)} %get-tuple-element.81, s32[768]{0:T(1024)S(1)} %get-tuple-element.77, s32[768]{0:T(1024)S(1)} %get-tuple-element.80, ...), kind=kLoop, calls=%fused_computation.3 | loop fusion | flops 19906560 | bytes 4437504 | tf_op jit(solution)/shard_map/convert_element_type | solution.py:18
  49.0 17.9 %all-to-all-done = bf16[16,90,256]{2,1,0:T(8,128)(2,1)S(1)} async-done(((bf16[16,90,256]{2,1,0:T(8,128)(2,1)}), bf16[16,90,256]{2,1,0:T(8,128)(2,1)S(1)}, u32[]{:S(2)}, u32[]{:S(2)}) %all-to-all-start) | async-done | bytes 737312 | tf_op jit(solution)/shard_map/all_to_all | solution.py:44
  66.9 1.1 reshape.198
  68.0 2.7 %fusion.74 = f32[768,256]{1,0:T(8,128)S(1)} fusion(bf16[1440,768]{1,0:T(8,128)(2,1)} %get-tuple-element.7, bf16[1440,256]{1,0:T(8,128)(2,1)} %reshape.198), kind=kOutput, calls=%fused_computation.163 | convolution fusion | flops 566231040 | bytes 3735552 | tf_op jit(solution)/shard_map/dot_general | solution.py:22
  70.8 1.6 fusion.8
  72.4 3.6 %all-to-all-start.1 = ((bf16[16,48,256]{2,1,0:T(8,128)(2,1)}), bf16[16,48,256]{2,1,0:T(8,128)(2,1)S(1)}, u32[]{:S(2)}, u32[]{:S(2)}) async-start(bf16[16,48,256]{2,1,0:T(8,128)(2,1)} %bitcast), calls=%async_computation.1 | async-start | bytes 786432 | tf_op jit(solution)/shard_map/all_to_all | solution.py:46
  86.0 2.9 %stack.131 = bf16[32,16,384]{2,0,1:T(8,128)(2,1)S(1)} concatenate(bf16[1,16,384]{2,0,1:T(2,128)(2,1)} %copy.370, bf16[1,16,384]{2,0,1:T(2,128)(2,1)} %copy.371, bf16[1,16,384]{2,0,1:T(2,128)(2,1)} %copy.372, bf16[1,16,384]{2,0,1:T(2,128)(2,1)} %copy.373, bf16[1,16,384]{2,0,1:T(2,128)(2,1)} %copy.374, bf16[1,16,384]{2,0,1:T(2,128)(2,1)} %copy.375, bf16[1,16,384]{2,0,1:T(2,128)(2,1)} %copy.376, ...), dimensions={0} | concatenate | bytes 786432 | tf_op jit(solution)/shard_map/stack | solution.py:54
  88.9 12.7 %all-to-all-done.1 = bf16[16,48,256]{2,1,0:T(8,128)(2,1)S(1)} async-done(((bf16[16,48,256]{2,1,0:T(8,128)(2,1)}), bf16[16,48,256]{2,1,0:T(8,128)(2,1)S(1)}, u32[]{:S(2)}, u32[]{:S(2)}) %all-to-all-start.1) | async-done | bytes 393248 | tf_op jit(solution)/shard_map/all_to_all | solution.py:46
  101.9 1.3 copy.402
  103.2 8.2 %all-to-all-start.2 = ((bf16[32,16,768]{2,1,0:T(8,128)(2,1)}), bf16[32,16,768]{2,1,0:T(8,128)(2,1)S(1)}, u32[]{:S(2)}, u32[]{:S(2)}) async-start(bf16[32,16,768]{2,1,0:T(8,128)(2,1)} %copy.402), calls=%async_computation.2 | async-start | bytes 1572864 | tf_op jit(solution)/shard_map/all_to_all | solution.py:58
  111.6 40.1 %all-to-all-done.2 = bf16[32,16,768]{2,1,0:T(8,128)(2,1)S(1)} async-done(((bf16[32,16,768]{2,1,0:T(8,128)(2,1)}), bf16[32,16,768]{2,1,0:T(8,128)(2,1)S(1)}, u32[]{:S(2)}, u32[]{:S(2)}) %all-to-all-start.2) | async-done | bytes 786464 | tf_op jit(solution)/shard_map/all_to_all | solution.py:58
  152.8 1.1 copy.406
  153.9 1.1 copy.404
  155.0 0.9 broadcast_select_fusion
  155.9 1.6 fusion.9
  157.5 1.6 fusion.17
  159.8 29.6 %all_to_all.30 = bf16[32,16,384]{2,1,0:T(8,128)(2,1)S(1)} all-to-all(bf16[32,16,384]{2,1,0:T(8,128)(2,1)S(1)} %convert_element_type.83), channel_id=1, replica_groups=mesh['lat'=32,'lon'=16] {'lat'}, dimensions={0} | all-to-all | bytes 786432 | tf_op jit(solution)/shard_map/all_to_all | solution.py:96
  189.7 1.0 broadcast_in_dim.65
  190.7 3.8 %all-to-all-start.4 = ((bf16[16,2,48,256]{3,2,1,0:T(8,128)(2,1)}), bf16[16,2,48,256]{3,2,1,0:T(8,128)(2,1)S(1)}, u32[]{:S(2)}, u32[]{:S(2)}) async-start(bf16[16,2,48,256]{3,2,1,0:T(8,128)(2,1)} %bitcast.155), calls=%async_computation.4 | async-start | bytes 1572864 | tf_op jit(solution)/shard_map/all_to_all | solution.py:108
  194.5 4.1 %reshape.196 = bf16[4,2,2,90,768]{4,3,2,1,0:T(8,128)(2,1)} reshape(bf16[1440,768]{1,0:T(8,128)(2,1)} %get-tuple-element.7) | data formatting | bytes 4423680 | tf_op jit(solution)/shard_map/reshape | solution.py:111
  198.6 2.2 reshape.205
  200.8 1.3 constant_dynamic-slice_fusion.1
  202.2 1.2 reshape.209
  203.4 1.3 constant_dynamic-slice_fusion
  204.7 1.2 reshape.210
  205.9 36.0 %all-to-all-done.4 = bf16[16,2,48,256]{3,2,1,0:T(8,128)(2,1)S(1)} async-done(((bf16[16,2,48,256]{3,2,1,0:T(8,128)(2,1)}), bf16[16,2,48,256]{3,2,1,0:T(8,128)(2,1)S(1)}, u32[]{:S(2)}, u32[]{:S(2)}) %all-to-all-start.4) | async-done | bytes 786464 | tf_op jit(solution)/shard_map/all_to_all | solution.py:108
  242.0 2.1 fusion.75
  245.4 15.0 %all_to_all.31 = bf16[8,2,90,256]{3,1,2,0:T(2,128)(2,1)S(1)} all-to-all(bf16[8,2,90,256]{3,1,2,0:T(2,128)(2,1)S(1)} %bitcast.158), channel_id=1, replica_groups={{0,1,4,5,8,9,12,13},{2,3,6,7,10,11,14,15},{16,17,20,21,24,25,28,29},{18..., dimensions={0} | all-to-all | bytes 1474560 | tf_op jit(solution)/shard_map/all_to_all | solution.py:119
  262.1 1.3 copy.414
  (122 shorter events, 25.3 us)
Async XLA Ops:
  0.0 260.6 %copy-start = (bf16[256,256]{1,0:T(8,128)(2,1)S(1)}, bf16[256,256]{1,0:T(8,128)(2,1)}, u32[]{:S(2)}) copy-start(bf16[256,256]{1,0:T(8,128)(2,1)} %param.6) | copy-start | bytes 393220
  0.0 19.2 %copy-start.3 = (bf16[16,24,192]{2,1,0:T(8,128)(2,1)S(1)}, bf16[16,24,192]{2,1,0:T(8,128)(2,1)}, u32[]{:S(2)}) copy-start(bf16[16,24,192]{2,1,0:T(8,128)(2,1)} %param.5) | copy-start | bytes 442372
  2.3 64.6 %all-to-all-start = ((bf16[16,90,256]{2,1,0:T(8,128)(2,1)}), bf16[16,90,256]{2,1,0:T(8,128)(2,1)S(1)}, u32[]{:S(2)}, u32[]{:S(2)}) async-start(bf16[16,90,256]{2,1,0:T(8,128)(2,1)} %copy.345), calls=%async_computation | async-start | bytes 1572864 | tf_op jit(solution)/shard_map/all_to_all | solution.py:44
  68.0 2.7 %copy-start.4 = (bf16[1440,256]{1,0:T(8,128)(2,1)S(1)}, bf16[1440,256]{1,0:T(8,128)(2,1)}, u32[]{:S(2)}) copy-start(bf16[1440,256]{1,0:T(8,128)(2,1)} %reshape.198) | copy-start | bytes 2211844
  70.7 9.9 %copy-start.21 = (bf16[16,1,192]{2,1,0:T(2,128)(2,1)S(1)}, bf16[16,1,192]{2,1,0:T(2,128)(2,1)}, u32[]{:S(2)}) copy-start(bf16[16,1,192]{2,1,0:T(2,128)(2,1)} %get-tuple-element.35) | copy-start | bytes 18436
  70.7 15.2 %copy-start.6 = (bf16[1,16,384]{2,0,1:T(2,128)(2,1)S(1)}, bf16[1,16,384]{2,0,1:T(2,128)(2,1)}, u32[]{:S(2)}) copy-start(bf16[1,16,384]{2,0,1:T(2,128)(2,1)} %copy.379) | copy-start | bytes 36868
  70.7 15.2 %copy-start.7 = (bf16[1,16,384]{2,0,1:T(2,128)(2,1)S(1)}, bf16[1,16,384]{2,0,1:T(2,128)(2,1)}, u32[]{:S(2)}) copy-start(bf16[1,16,384]{2,0,1:T(2,128)(2,1)} %copy.380) | copy-start | bytes 36868
  70.7 15.1 %copy-start.8 = (bf16[1,16,384]{2,0,1:T(2,128)(2,1)S(1)}, bf16[1,16,384]{2,0,1:T(2,128)(2,1)}, u32[]{:S(2)}) copy-start(bf16[1,16,384]{2,0,1:T(2,128)(2,1)} %copy.381) | copy-start | bytes 36868
  70.7 15.1 %copy-start.9 = (bf16[1,16,384]{2,0,1:T(2,128)(2,1)S(1)}, bf16[1,16,384]{2,0,1:T(2,128)(2,1)}, u32[]{:S(2)}) copy-start(bf16[1,16,384]{2,0,1:T(2,128)(2,1)} %copy.382) | copy-start | bytes 36868
  70.7 15.1 %copy-start.10 = (bf16[1,16,384]{2,0,1:T(2,128)(2,1)S(1)}, bf16[1,16,384]{2,0,1:T(2,128)(2,1)}, u32[]{:S(2)}) copy-start(bf16[1,16,384]{2,0,1:T(2,128)(2,1)} %copy.383) | copy-start | bytes 36868
  70.7 15.1 %copy-start.11 = (bf16[1,16,384]{2,0,1:T(2,128)(2,1)S(1)}, bf16[1,16,384]{2,0,1:T(2,128)(2,1)}, u32[]{:S(2)}) copy-start(bf16[1,16,384]{2,0,1:T(2,128)(2,1)} %copy.384) | copy-start | bytes 36868
  70.7 15.1 %copy-start.12 = (bf16[1,16,384]{2,0,1:T(2,128)(2,1)S(1)}, bf16[1,16,384]{2,0,1:T(2,128)(2,1)}, u32[]{:S(2)}) copy-start(bf16[1,16,384]{2,0,1:T(2,128)(2,1)} %copy.385) | copy-start | bytes 36868
  70.7 15.1 %copy-start.13 = (bf16[1,16,384]{2,0,1:T(2,128)(2,1)S(1)}, bf16[1,16,384]{2,0,1:T(2,128)(2,1)}, u32[]{:S(2)}) copy-start(bf16[1,16,384]{2,0,1:T(2,128)(2,1)} %copy.386) | copy-start | bytes 36868
  70.8 15.1 %copy-start.14 = (bf16[1,16,384]{2,0,1:T(2,128)(2,1)S(1)}, bf16[1,16,384]{2,0,1:T(2,128)(2,1)}, u32[]{:S(2)}) copy-start(bf16[1,16,384]{2,0,1:T(2,128)(2,1)} %copy.387) | copy-start | bytes 36868
  70.8 15.1 %copy-start.15 = (bf16[1,16,384]{2,0,1:T(2,128)(2,1)S(1)}, bf16[1,16,384]{2,0,1:T(2,128)(2,1)}, u32[]{:S(2)}) copy-start(bf16[1,16,384]{2,0,1:T(2,128)(2,1)} %copy.388) | copy-start | bytes 36868
  70.8 15.1 %copy-start.16 = (bf16[1,16,384]{2,0,1:T(2,128)(2,1)S(1)}, bf16[1,16,384]{2,0,1:T(2,128)(2,1)}, u32[]{:S(2)}) copy-start(bf16[1,16,384]{2,0,1:T(2,128)(2,1)} %copy.389) | copy-start | bytes 36868
  70.8 15.1 %copy-start.17 = (bf16[1,16,384]{2,0,1:T(2,128)(2,1)S(1)}, bf16[1,16,384]{2,0,1:T(2,128)(2,1)}, u32[]{:S(2)}) copy-start(bf16[1,16,384]{2,0,1:T(2,128)(2,1)} %copy.390) | copy-start | bytes 36868
  70.8 15.1 %copy-start.18 = (bf16[1,16,384]{2,0,1:T(2,128)(2,1)S(1)}, bf16[1,16,384]{2,0,1:T(2,128)(2,1)}, u32[]{:S(2)}) copy-start(bf16[1,16,384]{2,0,1:T(2,128)(2,1)} %copy.391) | copy-start | bytes 36868
  70.8 15.1 %copy-start.19 = (bf16[1,16,384]{2,0,1:T(2,128)(2,1)S(1)}, bf16[1,16,384]{2,0,1:T(2,128)(2,1)}, u32[]{:S(2)}) copy-start(bf16[1,16,384]{2,0,1:T(2,128)(2,1)} %copy.392) | copy-start | bytes 36868
  70.8 15.1 %copy-start.20 = (bf16[1,16,384]{2,0,1:T(2,128)(2,1)S(1)}, bf16[1,16,384]{2,0,1:T(2,128)(2,1)}, u32[]{:S(2)}) copy-start(bf16[1,16,384]{2,0,1:T(2,128)(2,1)} %copy.393) | copy-start | bytes 36868
  72.4 29.2 %all-to-all-start.1 = ((bf16[16,48,256]{2,1,0:T(8,128)(2,1)}), bf16[16,48,256]{2,1,0:T(8,128)(2,1)S(1)}, u32[]{:S(2)}, u32[]{:S(2)}) async-start(bf16[16,48,256]{2,1,0:T(8,128)(2,1)} %bitcast), calls=%async_computation.1 | async-start | bytes 786432 | tf_op jit(solution)/shard_map/all_to_all | solution.py:46
  103.2 48.5 %all-to-all-start.2 = ((bf16[32,16,768]{2,1,0:T(8,128)(2,1)}), bf16[32,16,768]{2,1,0:T(8,128)(2,1)S(1)}, u32[]{:S(2)}, u32[]{:S(2)}) async-start(bf16[32,16,768]{2,1,0:T(8,128)(2,1)} %copy.402), calls=%async_computation.2 | async-start | bytes 1572864 | tf_op jit(solution)/shard_map/all_to_all | solution.py:58
  190.7 51.3 %all-to-all-start.4 = ((bf16[16,2,48,256]{3,2,1,0:T(8,128)(2,1)}), bf16[16,2,48,256]{3,2,1,0:T(8,128)(2,1)S(1)}, u32[]{:S(2)}, u32[]{:S(2)}) async-start(bf16[16,2,48,256]{3,2,1,0:T(8,128)(2,1)} %bitcast.155), calls=%async_computation.4 | async-start | bytes 1572864 | tf_op jit(solution)/shard_map/all_to_all | solution.py:108
  242.0 2.1 copy-start.2
  260.5 1.1 copy-start.1
  260.5 1.1 copy-start.5

commit v3 on v2

--- a/solution.py
+++ b/solution.py
@@ -8,10 +8,9 @@
 from jax.sharding import PartitionSpec as P
 
 
-def fourier_table(count_lon, count_wave):
-    longitude = lax.broadcasted_iota(jnp.int32, (count_lon, 2 * count_wave), 0)
-    column = lax.broadcasted_iota(jnp.int32, (count_lon, 2 * count_wave), 1)
-    phases = (longitude * (column // 2) + (count_lon // 4) * (column % 2)) % count_lon
+def fourier_table(longitude, count_lon, count_wave):
+    column = lax.broadcasted_iota(jnp.int32, (longitude.shape[0], 2 * count_wave), 1)
+    phases = (longitude[:, None] * (column // 2) + (count_lon // 4) * (column % 2)) % count_lon
     angles = phases.astype(jnp.float32) * (2.0 * math.pi / count_lon)
     table = math.sqrt(2.0 / count_lon) * jnp.cos(angles)
     high = lax.reduce_precision(table, exponent_bits=8, mantissa_bits=7)
@@ -38,14 +37,30 @@
     half_deg = legendre.shape[2]
     all_rows = lat_rows * lat_count
     half_rows = all_rows // 2
-    table_hi, table_lo = fourier_table(count_lon, wave_dev * lon_count)
     skip_term = jnp.einsum("rlc,dc->rld", cotangent, skip_weight, preferred_element_type=jnp.float32)
 
-    row_grid = lax.all_to_all(cotangent, "lon", 0, 0, tiled=True).reshape(count_lon, width)
-    spectra = split_dot(table_hi, table_lo, row_grid, (((0,), (0,)), ((), ())))
-    coeffs = lax.all_to_all(
-        spectra.astype(jnp.bfloat16).reshape(lon_count, 2 * wave_dev, width), "lon", 0, 0, tiled=True
-    )
+    halves = 2
+    group = lon_count // halves
+    pair_rows = lat_rows // group
+    own_half = (lax.axis_index("lon") // 2) % halves
+    position = jnp.arange(group * lon_dev) // lon_dev
+    longitude = lon_dev * ((position // 2) * 4 + 2 * own_half + position % 2) + jnp.arange(
+        group * lon_dev
+    ) % lon_dev
+    table_hi, table_lo = fourier_table(longitude, count_lon, wave_dev * lon_count)
+    lon_ids = np.arange(lon_count).reshape(lon_count // 4, halves, 2)
+    half_groups = [lon_ids[:, h, :].reshape(-1).tolist() for h in range(halves)]
+
+    pair_grid = lax.all_to_all(
+        cotangent.reshape(group, pair_rows, lon_dev, width), "lon", 0, 0, tiled=True,
+        axis_index_groups=half_groups,
+    ).transpose(1, 0, 2, 3).reshape(pair_rows, group * lon_dev, width)
+    partial = split_dot(table_hi, table_lo, pair_grid, (((0,), (1,)), ((), ())))
+    partial_recv = lax.all_to_all(
+        partial.astype(jnp.bfloat16).reshape(lon_count, 2 * wave_dev, pair_rows, width), "lon", 0, 0, tiled=True
+    ).reshape(lon_count // 4, halves, 2, 2 * wave_dev, pair_rows, width)
+    coeffs = jnp.sum(partial_recv.astype(jnp.float32), axis=1).astype(jnp.bfloat16)
+    coeffs = coeffs.transpose(0, 1, 3, 2, 4).reshape(lat_rows, 2 * wave_dev, width)
     units_total = wave_dev * 4
     units_per_dev = units_total // lat_count
     unit_width = width // 2
@@ -97,25 +112,14 @@
         grad_units.reshape(lat_count, lat_rows, units_per_dev * unit_width), "lat", 0, 0, tiled=True
     ).transpose(1, 0, 2).reshape(lat_rows, 2 * wave_dev, width)
 
-    halves = 2
-    group = lon_count // halves
-    pair_rows = lat_rows // group
-    own_half = (lax.axis_index("lon") // 2) % halves
     by_pair = returned.reshape(lon_count // 4, 1, 2, pair_rows, 2 * wave_dev, width)
     pair_send = jnp.broadcast_to(
         by_pair, (lon_count // 4, halves, 2, pair_rows, 2 * wave_dev, width)
     ).reshape(lon_count, pair_rows, 2 * wave_dev, width)
     pair_coeffs = lax.all_to_all(pair_send, "lon", 0, 0, tiled=True)
     pair_coeffs = pair_coeffs.transpose(1, 0, 2, 3).reshape(pair_rows, 2 * wave_dev * lon_count, width)
-    half_table = lambda t: lax.dynamic_index_in_dim(
-        t.reshape(lon_count // 4, halves, 2, lon_dev, -1), own_half, axis=1, keepdims=False
-    ).reshape(group * lon_dev, -1)
-    half_grid = split_dot(
-        half_table(table_hi), half_table(table_lo), pair_coeffs, (((1,), (1,)), ((), ()))
-    )
+    half_grid = split_dot(table_hi, table_lo, pair_coeffs, (((1,), (1,)), ((), ())))
     half_send = half_grid.astype(jnp.bfloat16).reshape(group, lon_dev, pair_rows, width).transpose(0, 2, 1, 3)
-    lon_ids = np.arange(lon_count).reshape(lon_count // 4, halves, 2)
-    half_groups = [lon_ids[:, h, :].reshape(-1).tolist() for h in range(halves)]
     spatial = lax.all_to_all(
         half_send, "lon", 0, 0, tiled=True, axis_index_groups=half_groups
     ).reshape(lat_rows, lon_dev, width)

time: 264 us -> 243 us (0.920)
  blocking collectives: 44.6 us -> 95.2 us
  local copies, waits for them, and re-layouts: 46.2 us -> 15.9 us
  waiting for transfers between devices: 107 us -> 84 us
  other arithmetic: 21.6 us -> 10.9 us
  matrix products: 11.2 us -> 5.11 us
    all_to_all x0 -> x1, blocking collectives: none -> 50.6 us  [shards(): pair_coeffs = lax.all_to_all(pair_send, 'lon', 0, 0, tiled=True)]
    all_to_all x3 -> x2, waiting for transfers between devices: 66.6 us -> 44.7 us  [the longest x1 44.7 us: shards(): lax.all_to_all(partial.astype(jnp.bfloat16).reshape(lon_count, 2 * wave_d...]
    another operation x33, local copies, waits for them, and re-layouts: 21.8 us -> 4.39 us  [shards(): jnp.stack([jnp.concatenate([legendre[:, a], legendre[:, b]], axis=-1) for...]
    convert_element_type x1, other arithmetic: 19 us -> 9.52 us  [fourier_table(): (table - high).astype(jnp.bfloat16)]
    reshape x6 -> x3, local copies, waits for them, and re-layouts: 10 us -> 4.46 us  [the longest x2 3.49 us: shards(): cotangent.reshape(group, pair_rows, lon_dev, width)]
    dot_general x4, matrix products: 7.04 us -> 3.1 us  [split_dot(): lax.dot_general(t, values, dims, preferred_element_type=jnp.float32)]
    dynamic_slice x2 -> x0, local copies, waits for them, and re-layouts: 2.69 us -> none  [shards(): lax.dynamic_index_in_dim(t.reshape(lon_count // 4, halves, 2, lon_dev, -1...]
    all_to_all x3 -> x2, starting transfers between devices: 24.3 us -> 22 us  [the longest x1 17.4 us: shards(): lax.all_to_all(partial.astype(jnp.bfloat16).reshape(lon_count, 2 * wave_d...]
  transfers between devices with their start and end apart: 4 -> 3, of which waited for: 4 -> 2; matrix products, arithmetic and copies ran while one was open for 21% -> 7% of each run, Pallas kernels for 0% -> 0%
where the time goes in v3:
time: 243 us; the launch traced here: 242 us
  blocking collectives  95.2 us (39%)
  waiting for transfers between devices  84 us (35%)
  starting transfers between devices  30.2 us (12%)
  local copies, waits for them, and re-layouts  15.9 us (7%)
  other arithmetic  10.9 us (4%)
  matrix products  5.11 us (2%)
    all_to_all x1, blocking collectives, shards(): pair_coeffs = lax.all_to_all(pair_send, 'lon', 0, 0, tiled=True)  50.6 us
    all_to_all x1, waiting for transfers between devices, shards(): lax.all_to_all(partial.astype(jnp.bfloat16).reshape(lon_count, 2 * wave_d...  44.7 us
    all_to_all x1, waiting for transfers between devices, shards(): lax.all_to_all(payload, 'lat', 0, 0, tiled=True).reshape(all_rows, -1)  39.3 us
    all_to_all x1, blocking collectives, shards(): lax.all_to_all(grad_units.reshape(lat_count, lat_rows, units_per_dev * un...  29.6 us
    all_to_all x1, starting transfers between devices, shards(): lax.all_to_all(partial.astype(jnp.bfloat16).reshape(lon_count, 2 * wave_d...  17.4 us
    all_to_all x1, blocking collectives, shards(): lax.all_to_all(half_send, 'lon', 0, 0, tiled=True, axis_index_groups=half...  15 us
    convert_element_type x1, other arithmetic, fourier_table(): (table - high).astype(jnp.bfloat16)  9.52 us
    all_to_all x1, starting transfers between devices, shards(): lax.all_to_all(payload, 'lat', 0, 0, tiled=True).reshape(all_rows, -1)  8.18 us
  transfers between devices with their start and end apart: 3, of which 2 were waited for; matrix products, arithmetic and copies ran while one was open for 7% of the time, Pallas kernels for 0%

profile of v3, /device:TPU:32, one launch (start us, length us, event | category | flops | bytes accessed | tf_op | source)
XLA Modules:
  0.0 242.0 jit_solution(7547220680753298325)
XLA Ops:
  0.0 2.1 reshape.234
  2.1 1.4 copy.356
  3.5 4.6 %all-to-all-start = ((bf16[8,2,90,256]{3,1,2,0:T(2,128)(2,1)}), bf16[8,2,90,256]{3,1,2,0:T(2,128)(2,1)S(1)}, u32[]{:S(2)}, u32[]{:S(2)}) async-start(bf16[8,2,90,256]{3,1,2,0:T(2,128)(2,1)} %copy.356), calls=%async_computation | async-start | bytes 1474560 | tf_op jit(solution)/shard_map/all_to_all | solution.py:54
  8.2 9.5 %fusion = (bf16[720,768]{1,0:T(8,128)(2,1)S(1)}, bf16[720,768]{1,0:T(8,128)(2,1)S(1)}) fusion(s32[768]{0:T(1024)S(1)} %get-tuple-element.100, s32[768]{0:T(1024)S(1)} %get-tuple-element.101, pred[768]{0:T(1024)(128)(4,1)S(1)} %get-tuple-element.103, s32[768]{0:T(1024)S(1)} %get-tuple-element.99, s32[768]{0:T(1024)S(1)} %get-tuple-element.102, ...), kind=kLoop, calls=%fused_computation.3 | loop fusion | flops 9953280 | bytes 2228544 | tf_op jit(solution)/shard_map/convert_element_type | solution.py:17
  17.7 1.0 fusion.95
  18.8 0.6 copy.414
  19.5 0.6 copy.415
  20.1 0.6 copy.416
  20.7 0.6 copy.417
  21.3 0.8 fusion.14
  22.1 0.8 add_convert_fusion.1
  23.0 1.0 copy.359
  24.0 17.4 %all-to-all-start.1 = ((bf16[16,48,2,256]{3,1,2,0:T(8,128)(2,1)}), bf16[16,48,2,256]{3,1,2,0:T(8,128)(2,1)S(1)}, u32[]{:S(2)}, u32[]{:S(2)}) async-start(bf16[16,48,2,256]{3,1,2,0:T(8,128)(2,1)} %copy.359), calls=%async_computation.1 | async-start | bytes 1572864 | tf_op jit(solution)/shard_map/all_to_all | solution.py:59
  43.0 1.3 stack.131
  44.3 44.7 %all-to-all-done.1 = bf16[16,48,2,256]{3,1,2,0:T(8,128)(2,1)S(1)} async-done(((bf16[16,48,2,256]{3,1,2,0:T(8,128)(2,1)}), bf16[16,48,2,256]{3,1,2,0:T(8,128)(2,1)S(1)}, u32[]{:S(2)}, u32[]{:S(2)}) %all-to-all-start.1) | async-done | bytes 786464 | tf_op jit(solution)/shard_map/all_to_all | solution.py:59
  89.6 1.3 copy.418
  91.0 8.2 %all-to-all-start.2 = ((bf16[32,16,768]{2,1,0:T(8,128)(2,1)}), bf16[32,16,768]{2,1,0:T(8,128)(2,1)S(1)}, u32[]{:S(2)}, u32[]{:S(2)}) async-start(bf16[32,16,768]{2,1,0:T(8,128)(2,1)} %copy.418), calls=%async_computation.2 | async-start | bytes 1572864 | tf_op jit(solution)/shard_map/all_to_all | solution.py:73
  99.3 39.3 %all-to-all-done.2 = bf16[32,16,768]{2,1,0:T(8,128)(2,1)S(1)} async-done(((bf16[32,16,768]{2,1,0:T(8,128)(2,1)}), bf16[32,16,768]{2,1,0:T(8,128)(2,1)S(1)}, u32[]{:S(2)}, u32[]{:S(2)}) %all-to-all-start.2) | async-done | bytes 786464 | tf_op jit(solution)/shard_map/all_to_all | solution.py:73
  139.3 0.5 fusion.8
  139.9 0.5 fusion.25
  140.5 0.3 copy.424
  140.8 0.3 convert_element_type.83
  141.1 29.6 %all_to_all.30 = bf16[32,16,384]{2,1,0:T(8,128)(2,1)S(1)} all-to-all(bf16[32,16,384]{2,1,0:T(8,128)(2,1)S(1)} %convert_element_type.83), channel_id=1, replica_groups=mesh['lat'=32,'lon'=16] {'lat'}, dimensions={0} | all-to-all | bytes 786432 | tf_op jit(solution)/shard_map/all_to_all | solution.py:111
  171.2 50.6 %all_to_all.31 = bf16[16,2,48,256]{3,2,1,0:T(8,128)(2,1)S(1)} all-to-all(bf16[16,2,48,256]{3,2,1,0:T(8,128)(2,1)S(1)} %bitcast.171), channel_id=1, replica_groups=mesh['lat'=32,'lon'=16] {'lon'}, dimensions={0} | all-to-all | bytes 1572864 | tf_op jit(solution)/shard_map/all_to_all | solution.py:119
  221.8 0.7 fusion.12
  222.6 0.7 add_convert_fusion.2
  223.3 0.6 copy.427
  223.9 15.0 %all_to_all.32 = bf16[8,2,90,256]{3,1,2,0:T(2,128)(2,1)S(1)} all-to-all(bf16[8,2,90,256]{3,1,2,0:T(2,128)(2,1)S(1)} %bitcast.173), channel_id=1, replica_groups={{0,1,4,5,8,9,12,13},{2,3,6,7,10,11,14,15},{16,17,20,21,24,25,28,29},{18..., dimensions={0} | all-to-all | bytes 1474560 | tf_op jit(solution)/shard_map/all_to_all | solution.py:123
  239.1 0.4 fusion.32
  239.5 0.7 copy-done.1
  240.2 0.5 add_convert_fusion
  240.7 1.3 copy.430
  (96 shorter events, 3.5 us)
Async XLA Ops:
  0.0 239.1 %copy-start = (bf16[256,256]{1,0:T(8,128)(2,1)S(1)}, bf16[256,256]{1,0:T(8,128)(2,1)}, u32[]{:S(2)}) copy-start(bf16[256,256]{1,0:T(8,128)(2,1)} %param.6) | copy-start | bytes 393220
  3.5 14.2 %copy-start.4 = (bf16[16,24,192]{2,1,0:T(8,128)(2,1)S(1)}, bf16[16,24,192]{2,1,0:T(8,128)(2,1)}, u32[]{:S(2)}) copy-start(bf16[16,24,192]{2,1,0:T(8,128)(2,1)} %param.5) | copy-start | bytes 442372
  3.5 17.8 %all-to-all-start = ((bf16[8,2,90,256]{3,1,2,0:T(2,128)(2,1)}), bf16[8,2,90,256]{3,1,2,0:T(2,128)(2,1)S(1)}, u32[]{:S(2)}, u32[]{:S(2)}) async-start(bf16[8,2,90,256]{3,1,2,0:T(2,128)(2,1)} %copy.356), calls=%async_computation | async-start | bytes 1474560 | tf_op jit(solution)/shard_map/all_to_all | solution.py:54
  17.7 4.4 %copy-start.2 = (bf16[720,768]{1,0:T(8,128)(2,1)}, bf16[720,768]{1,0:T(8,128)(2,1)S(1)}, u32[]{:S(2)}) copy-start(bf16[720,768]{1,0:T(8,128)(2,1)S(1)} %get-tuple-element.7) | copy-start | bytes 3317764
  23.9 18.5 %copy-start.10 = (bf16[16,1,192]{2,1,0:T(2,128)(2,1)S(1)}, bf16[16,1,192]{2,1,0:T(2,128)(2,1)}, u32[]{:S(2)}) copy-start(bf16[16,1,192]{2,1,0:T(2,128)(2,1)} %get-tuple-element.35) | copy-start | bytes 18436
  23.9 19.0 %copy-start.6 = (bf16[1,16,384]{2,0,1:T(2,128)(2,1)S(1)}, bf16[1,16,384]{2,0,1:T(2,128)(2,1)}, u32[]{:S(2)}) copy-start(bf16[1,16,384]{2,0,1:T(2,128)(2,1)} %copy.414) | copy-start | bytes 36868
  23.9 19.0 %copy-start.7 = (bf16[1,16,384]{2,0,1:T(2,128)(2,1)S(1)}, bf16[1,16,384]{2,0,1:T(2,128)(2,1)}, u32[]{:S(2)}) copy-start(bf16[1,16,384]{2,0,1:T(2,128)(2,1)} %copy.415) | copy-start | bytes 36868
  23.9 19.0 %copy-start.8 = (bf16[1,16,384]{2,0,1:T(2,128)(2,1)S(1)}, bf16[1,16,384]{2,0,1:T(2,128)(2,1)}, u32[]{:S(2)}) copy-start(bf16[1,16,384]{2,0,1:T(2,128)(2,1)} %copy.416) | copy-start | bytes 36868
  23.9 19.0 %copy-start.9 = (bf16[1,16,384]{2,0,1:T(2,128)(2,1)S(1)}, bf16[1,16,384]{2,0,1:T(2,128)(2,1)}, u32[]{:S(2)}) copy-start(bf16[1,16,384]{2,0,1:T(2,128)(2,1)} %copy.417) | copy-start | bytes 36868
  24.0 65.1 %all-to-all-start.1 = ((bf16[16,48,2,256]{3,1,2,0:T(8,128)(2,1)}), bf16[16,48,2,256]{3,1,2,0:T(8,128)(2,1)S(1)}, u32[]{:S(2)}, u32[]{:S(2)}) async-start(bf16[16,48,2,256]{3,1,2,0:T(8,128)(2,1)} %copy.359), calls=%async_computation.1 | async-start | bytes 1572864 | tf_op jit(solution)/shard_map/all_to_all | solution.py:59
  91.0 47.6 %all-to-all-start.2 = ((bf16[32,16,768]{2,1,0:T(8,128)(2,1)}), bf16[32,16,768]{2,1,0:T(8,128)(2,1)S(1)}, u32[]{:S(2)}, u32[]{:S(2)}) async-start(bf16[32,16,768]{2,1,0:T(8,128)(2,1)} %copy.418), calls=%async_computation.2 | async-start | bytes 1572864 | tf_op jit(solution)/shard_map/all_to_all | solution.py:73
  171.2 50.7 %copy-start.3 = (bf16[720,768]{1,0:T(8,128)(2,1)S(1)}, bf16[720,768]{1,0:T(8,128)(2,1)}, u32[]{:S(2)}) copy-start(bf16[720,768]{1,0:T(8,128)(2,1)} %copy-done.2) | copy-start | bytes 3317764
  239.1 1.1 copy-start.1
  239.1 1.1 copy-start.5

commit v4 on v3

--- a/solution.py
+++ b/solution.py
@@ -37,6 +37,14 @@
     half_deg = legendre.shape[2]
     all_rows = lat_rows * lat_count
     half_rows = all_rows // 2
+    units_total = wave_dev * 4
+    units_per_dev = units_total // lat_count
+    slots = unit_slots(lat_count, units_per_dev)
+    basis_send = jnp.stack(
+        [jnp.concatenate([legendre[:, a], legendre[:, b]], axis=-1) for a, b in slots.tolist()]
+    )
+    basis_recv = lax.all_to_all(basis_send, "lat", 0, 0, tiled=True).reshape(all_rows, 2, half_deg)
+    basis_recv, cotangent_held = lax.optimization_barrier((basis_recv, cotangent))
     skip_term = jnp.einsum("rlc,dc->rld", cotangent, skip_weight, preferred_element_type=jnp.float32)
 
     halves = 2
@@ -52,7 +60,7 @@
     half_groups = [lon_ids[:, h, :].reshape(-1).tolist() for h in range(halves)]
 
     pair_grid = lax.all_to_all(
-        cotangent.reshape(group, pair_rows, lon_dev, width), "lon", 0, 0, tiled=True,
+        cotangent_held.reshape(group, pair_rows, lon_dev, width), "lon", 0, 0, tiled=True,
         axis_index_groups=half_groups,
     ).transpose(1, 0, 2, 3).reshape(pair_rows, group * lon_dev, width)
     partial = split_dot(table_hi, table_lo, pair_grid, (((0,), (1,)), ((), ())))
@@ -61,18 +69,10 @@
     ).reshape(lon_count // 4, halves, 2, 2 * wave_dev, pair_rows, width)
     coeffs = jnp.sum(partial_recv.astype(jnp.float32), axis=1).astype(jnp.bfloat16)
     coeffs = coeffs.transpose(0, 1, 3, 2, 4).reshape(lat_rows, 2 * wave_dev, width)
-    units_total = wave_dev * 4
-    units_per_dev = units_total // lat_count
     unit_width = width // 2
     unit_send = coeffs.reshape(lat_rows, lat_count, units_per_dev * unit_width).transpose(1, 0, 2)
-    slots = unit_slots(lat_count, units_per_dev)
-    basis_send = jnp.stack(
-        [jnp.concatenate([legendre[:, a], legendre[:, b]], axis=-1) for a, b in slots.tolist()]
-    )
-    payload = jnp.concatenate([unit_send, basis_send], axis=-1)
-    arrived = lax.all_to_all(payload, "lat", 0, 0, tiled=True).reshape(all_rows, -1)
-    gathered = arrived[:, : units_per_dev * unit_width].reshape(all_rows, units_per_dev, unit_width)
-    basis_recv = arrived[:, units_per_dev * unit_width :].reshape(all_rows, 2, half_deg)
+    arrived = lax.all_to_all(unit_send, "lat", 0, 0, tiled=True).reshape(all_rows, -1)
+    gathered = arrived.reshape(all_rows, units_per_dev, unit_width)
 
     band = lax.axis_index("lat")
     unit_ids = units_per_dev * band + jnp.arange(units_per_dev)

time: 243 us -> 275 us (1.13)
  blocking collectives: 95.2 us -> 152 us
  waiting for transfers between devices: 84 us -> 46.7 us
  other arithmetic: 10.9 us -> 32.5 us
  starting transfers between devices: 30.2 us -> 25.2 us
  local copies, waits for them, and re-layouts: 15.9 us -> 12.1 us
    all_to_all x0 -> x1, blocking collectives: none -> 56.2 us  [shards(): lax.all_to_all(partial.astype(jnp.bfloat16).reshape(lon_count, 2 * wave_d...]
    all_to_all x3, waiting for transfers between devices: 84 us -> 46.7 us  [the longest x1 23.1 us: shards(): lax.all_to_all(basis_send, 'lat', 0, 0, tiled=True)]
    unnamed x0 -> x31, other arithmetic: none -> 21 us
    all_to_all x3, starting transfers between devices: 30.2 us -> 25.2 us  [the longest x1 15.2 us: shards(): lax.all_to_all(basis_send, 'lat', 0, 0, tiled=True)]
    another operation x33 -> x0, local copies, waits for them, and re-layouts: 4.39 us -> none  [shards(): jnp.stack([jnp.concatenate([legendre[:, a], legendre[:, b]], axis=-1) for...]
  transfers between devices with their start and end apart: 3 -> 3, of which waited for: 2 -> 3; matrix products, arithmetic and copies ran while one was open for 7% -> 4% of each run, Pallas kernels for 0% -> 0%
where the time goes in v4:
time: 275 us
  blocking collectives  152 us (55%)
  waiting for transfers between devices  46.7 us (17%)
  other arithmetic  32.5 us (12%)
  starting transfers between devices  25.2 us (9%)
  local copies, waits for them, and re-layouts  12.1 us (4%)
  matrix products  6.36 us (2%)
    all_to_all x1, blocking collectives, shards(): lax.all_to_all(partial.astype(jnp.bfloat16).reshape(lon_count, 2 * wave_d...  56.2 us
    all_to_all x1, blocking collectives, shards(): pair_coeffs = lax.all_to_all(pair_send, 'lon', 0, 0, tiled=True)  50.6 us
    all_to_all x1, blocking collectives, shards(): lax.all_to_all(grad_units.reshape(lat_count, lat_rows, units_per_dev * un...  29.7 us
    all_to_all x1, waiting for transfers between devices, shards(): lax.all_to_all(basis_send, 'lat', 0, 0, tiled=True)  23.1 us
    all_to_all x1, waiting for transfers between devices, shards(): lax.all_to_all(unit_send, 'lat', 0, 0, tiled=True).reshape(all_rows, -1)  21.3 us
    unnamed x31, other arithmetic  21 us
    all_to_all x1, starting transfers between devices, shards(): lax.all_to_all(basis_send, 'lat', 0, 0, tiled=True)  15.2 us
    all_to_all x1, blocking collectives, shards(): lax.all_to_all(half_send, 'lon', 0, 0, tiled=True, axis_index_groups=half...  15 us
  transfers between devices with their start and end apart: 3, of which 3 were waited for; matrix products, arithmetic and copies ran while one was open for 4% of the time, Pallas kernels for 0%

profile of v4, /device:TPU:32, one launch (start us, length us, event | category | flops | bytes accessed | tf_op | source)
XLA Modules:
  0.0 274.7 jit_solution(5529894549503882451)
XLA Ops:
  0.0 1.1 fusion.101
  1.1 2.2 fusion.100
  4.0 0.7 constant_dynamic-update-slice_fusion.30
  6.1 0.7 constant_dynamic-update-slice_fusion.27
  8.8 0.7 constant_dynamic-update-slice_fusion.23
  10.2 0.7 constant_dynamic-update-slice_fusion.21
  12.2 0.7 constant_dynamic-update-slice_fusion.18
  14.2 0.7 constant_dynamic-update-slice_fusion.15
  15.6 0.7 constant_dynamic-update-slice_fusion.13
  17.6 0.7 constant_dynamic-update-slice_fusion.10
  19.7 0.7 constant_dynamic-update-slice_fusion.7
  21.0 0.7 constant_dynamic-update-slice_fusion.5
  23.1 0.7 constant_dynamic-update-slice_fusion.2
  25.1 15.2 %all-to-all-start = ((bf16[32,16,384]{2,1,0:T(8,128)(2,1)}), bf16[32,16,384]{2,1,0:T(8,128)(2,1)S(1)}, u32[]{:S(2)}, u32[]{:S(2)}) async-start(bf16[32,16,384]{2,1,0:T(8,128)(2,1)} %constant_dynamic-update-slice_fusion), calls=%async_computation | async-start | bytes 786432 | tf_op jit(solution)/shard_map/all_to_all | solution.py:46
  40.4 23.1 %all-to-all-done = bf16[32,16,384]{2,1,0:T(8,128)(2,1)S(1)} async-done(((bf16[32,16,384]{2,1,0:T(8,128)(2,1)}), bf16[32,16,384]{2,1,0:T(8,128)(2,1)S(1)}, u32[]{:S(2)}, u32[]{:S(2)}) %all-to-all-start) | async-done | bytes 393248 | tf_op jit(solution)/shard_map/all_to_all | solution.py:46
  64.1 1.4 copy.98
  65.4 4.5 %all-to-all-start.1 = ((bf16[8,2,90,256]{3,1,2,0:T(2,128)(2,1)}), bf16[8,2,90,256]{3,1,2,0:T(2,128)(2,1)S(1)}, u32[]{:S(2)}, u32[]{:S(2)}) async-start(bf16[8,2,90,256]{3,1,2,0:T(2,128)(2,1)} %copy.98), calls=%async_computation.1 | async-start | bytes 1474560 | tf_op jit(solution)/shard_map/all_to_all | solution.py:62
  69.9 10.2 %fusion = (bf16[720,768]{1,0:T(8,128)(2,1)S(1)}, bf16[720,768]{1,0:T(8,128)(2,1)}) fusion(s32[768]{0:T(1024)S(1)} %get-tuple-element.74, s32[768]{0:T(1024)S(1)} %get-tuple-element.75, pred[768]{0:T(1024)(128)(4,1)S(1)} %get-tuple-element.77, s32[768]{0:T(1024)S(1)} %get-tuple-element.73, s32[768]{0:T(1024)S(1)} %get-tuple-element.76, ...), kind=kLoop, calls=%fused_computation.3 | loop fusion | flops 9953280 | bytes 2228544 | tf_op jit(solution)/shard_map/convert_element_type | solution.py:17
  80.1 2.4 all-to-all-done.1
  82.5 2.1 fusion.14
  84.6 0.8 add_convert_fusion.1
  85.5 56.2 %all_to_all.35 = bf16[16,48,2,256]{3,1,2,0:T(8,128)(2,1)S(1)} all-to-all(bf16[16,48,2,256]{3,1,2,0:T(8,128)(2,1)S(1)} %copy.101), channel_id=1, replica_groups=mesh['lat'=32,'lon'=16] {'lon'}, dimensions={0} | all-to-all | bytes 1572864 | tf_op jit(solution)/shard_map/all_to_all | solution.py:67
  142.1 0.9 copy.104
  143.0 5.5 %all-to-all-start.3 = ((bf16[32,16,384]{2,1,0:T(8,128)(2,1)}), bf16[32,16,384]{2,1,0:T(8,128)(2,1)S(1)}, u32[]{:S(2)}, u32[]{:S(2)}) async-start(bf16[32,16,384]{2,1,0:T(8,128)(2,1)} %copy.104), calls=%async_computation.3 | async-start | bytes 786432 | tf_op jit(solution)/shard_map/all_to_all | solution.py:74
  148.7 0.7 fusion.99
  150.2 21.3 %all-to-all-done.3 = bf16[32,16,384]{2,1,0:T(8,128)(2,1)S(1)} async-done(((bf16[32,16,384]{2,1,0:T(8,128)(2,1)}), bf16[32,16,384]{2,1,0:T(8,128)(2,1)S(1)}, u32[]{:S(2)}, u32[]{:S(2)}) %all-to-all-start.3) | async-done | bytes 393248 | tf_op jit(solution)/shard_map/all_to_all | solution.py:74
  173.5 29.7 %all_to_all.36 = bf16[32,16,384]{2,1,0:T(8,128)(2,1)S(1)} all-to-all(bf16[32,16,384]{2,1,0:T(8,128)(2,1)S(1)} %convert_element_type.83), channel_id=1, replica_groups=mesh['lat'=32,'lon'=16] {'lat'}, dimensions={0} | all-to-all | bytes 786432 | tf_op jit(solution)/shard_map/all_to_all | solution.py:111
  203.6 50.6 %all_to_all.37 = bf16[16,2,48,256]{3,2,1,0:T(8,128)(2,1)S(1)} all-to-all(bf16[16,2,48,256]{3,2,1,0:T(8,128)(2,1)S(1)} %bitcast.225), channel_id=1, replica_groups=mesh['lat'=32,'lon'=16] {'lon'}, dimensions={0} | all-to-all | bytes 1572864 | tf_op jit(solution)/shard_map/all_to_all | solution.py:119
  254.3 0.7 fusion.12
  255.5 0.7 add_convert_fusion.2
  256.8 15.0 %all_to_all.38 = bf16[8,2,90,256]{3,1,2,0:T(2,128)(2,1)S(1)} all-to-all(bf16[8,2,90,256]{3,1,2,0:T(2,128)(2,1)S(1)} %bitcast.227), channel_id=1, replica_groups={{0,1,4,5,8,9,12,13},{2,3,6,7,10,11,14,15},{16,17,20,21,24,25,28,29},{18..., dimensions={0} | all-to-all | bytes 1474560 | tf_op jit(solution)/shard_map/all_to_all | solution.py:123
  273.5 1.3 copy.113
  (78 shorter events, 21.3 us)
Async XLA Ops:
  0.0 272.0 %copy-start = (bf16[256,256]{1,0:T(8,128)(2,1)S(1)}, bf16[256,256]{1,0:T(8,128)(2,1)}, u32[]{:S(2)}) copy-start(bf16[256,256]{1,0:T(8,128)(2,1)} %param.6) | copy-start | bytes 393220
  4.0 59.7 %copy-start.1 = (bf16[16,90,256]{2,0,1:T(8,128)(2,1)S(1)}, bf16[16,90,256]{2,0,1:T(8,128)(2,1)}, u32[]{:S(2)}) copy-start(bf16[16,90,256]{2,0,1:T(8,128)(2,1)} %param.4) | copy-start | bytes 2211844
  25.1 38.4 %all-to-all-start = ((bf16[32,16,384]{2,1,0:T(8,128)(2,1)}), bf16[32,16,384]{2,1,0:T(8,128)(2,1)S(1)}, u32[]{:S(2)}, u32[]{:S(2)}) async-start(bf16[32,16,384]{2,1,0:T(8,128)(2,1)} %constant_dynamic-update-slice_fusion), calls=%async_computation | async-start | bytes 786432 | tf_op jit(solution)/shard_map/all_to_all | solution.py:46
  65.4 17.1 %all-to-all-start.1 = ((bf16[8,2,90,256]{3,1,2,0:T(2,128)(2,1)}), bf16[8,2,90,256]{3,1,2,0:T(2,128)(2,1)S(1)}, u32[]{:S(2)}, u32[]{:S(2)}) async-start(bf16[8,2,90,256]{3,1,2,0:T(2,128)(2,1)} %copy.98), calls=%async_computation.1 | async-start | bytes 1474560 | tf_op jit(solution)/shard_map/all_to_all | solution.py:62
  80.1 4.4 %copy-start.2 = (bf16[720,768]{1,0:T(8,128)(2,1)}, bf16[720,768]{1,0:T(8,128)(2,1)S(1)}, u32[]{:S(2)}) copy-start(bf16[720,768]{1,0:T(8,128)(2,1)S(1)} %get-tuple-element.12) | copy-start | bytes 3317764
  143.0 28.5 %all-to-all-start.3 = ((bf16[32,16,384]{2,1,0:T(8,128)(2,1)}), bf16[32,16,384]{2,1,0:T(8,128)(2,1)S(1)}, u32[]{:S(2)}, u32[]{:S(2)}) async-start(bf16[32,16,384]{2,1,0:T(8,128)(2,1)} %copy.104), calls=%async_computation.3 | async-start | bytes 786432 | tf_op jit(solution)/shard_map/all_to_all | solution.py:74
  203.6 50.7 %copy-start.4 = (bf16[720,768]{1,0:T(8,128)(2,1)S(1)}, bf16[720,768]{1,0:T(8,128)(2,1)}, u32[]{:S(2)}) copy-start(bf16[720,768]{1,0:T(8,128)(2,1)} %get-tuple-element.9) | copy-start | bytes 3317764
  254.3 1.2 copy-start.3
  272.0 0.9 copy-start.5

commit v5 on v3

--- a/solution.py
+++ b/solution.py
@@ -8,11 +8,24 @@
 from jax.sharding import PartitionSpec as P
 
 
-def fourier_table(longitude, count_lon, count_wave):
-    column = lax.broadcasted_iota(jnp.int32, (longitude.shape[0], 2 * count_wave), 1)
-    phases = (longitude[:, None] * (column // 2) + (count_lon // 4) * (column % 2)) % count_lon
-    angles = phases.astype(jnp.float32) * (2.0 * math.pi / count_lon)
-    table = math.sqrt(2.0 / count_lon) * jnp.cos(angles)
+def fourier_table(block, lon_dev, count_lon, count_wave):
+    column = lax.broadcasted_iota(jnp.int32, (1, 2 * count_wave), 1)
+    wavenum = column // 2
+
+    def turns(longitude):
+        phases = (longitude[:, None] * wavenum) % count_lon
+        angles = phases.astype(jnp.float32) * (2.0 * math.pi / count_lon)
+        return jnp.cos(angles), jnp.sin(angles)
+
+    block_cos, block_sin = turns(lon_dev * block)
+    inner_cos, inner_sin = turns(jnp.arange(lon_dev))
+    rows = block.shape[0] * lon_dev
+    block_cos, block_sin = (jnp.repeat(t, lon_dev, axis=0) for t in (block_cos, block_sin))
+    inner_cos, inner_sin = (jnp.tile(t, (block.shape[0], 1)) for t in (inner_cos, inner_sin))
+    cosine = block_cos * inner_cos - block_sin * inner_sin
+    sine = block_sin * inner_cos + block_cos * inner_sin
+    parity = jnp.broadcast_to(column % 2, (rows, 2 * count_wave))
+    table = math.sqrt(2.0 / count_lon) * jnp.where(parity == 0, cosine, -sine)
     high = lax.reduce_precision(table, exponent_bits=8, mantissa_bits=7)
     return lax.optimization_barrier((high.astype(jnp.bfloat16), (table - high).astype(jnp.bfloat16)))
 
@@ -43,11 +56,9 @@
     group = lon_count // halves
     pair_rows = lat_rows // group
     own_half = (lax.axis_index("lon") // 2) % halves
-    position = jnp.arange(group * lon_dev) // lon_dev
-    longitude = lon_dev * ((position // 2) * 4 + 2 * own_half + position % 2) + jnp.arange(
-        group * lon_dev
-    ) % lon_dev
-    table_hi, table_lo = fourier_table(longitude, count_lon, wave_dev * lon_count)
+    position = jnp.arange(group)
+    block = (position // 2) * 4 + 2 * own_half + position % 2
+    table_hi, table_lo = fourier_table(block, lon_dev, count_lon, wave_dev * lon_count)
     lon_ids = np.arange(lon_count).reshape(lon_count // 4, halves, 2)
     half_groups = [lon_ids[:, h, :].reshape(-1).tolist() for h in range(halves)]
 

time: 243 us -> 243 us (level)
  local copies, waits for them, and re-layouts: 15.9 us -> 20.2 us
  other arithmetic: 10.9 us -> 7.54 us
    convert_element_type x1, other arithmetic: 9.52 us -> 2.72 us  [fourier_table(): (table - high).astype(jnp.bfloat16)]
    neg x0 -> x1, local copies, waits for them, and re-layouts: none -> 2.78 us  [fourier_table(): table = math.sqrt(2.0 / count_lon) * jnp.where(parity == 0, cosine, -sine)]
where the time goes in v5:
time: 243 us
  blocking collectives  95.2 us (39%)
  waiting for transfers between devices  84 us (35%)
  starting transfers between devices  30.1 us (12%)
  local copies, waits for them, and re-layouts  20.2 us (8%)
  other arithmetic  7.54 us (3%)
  matrix products  5.12 us (2%)
    all_to_all x1, blocking collectives, shards(): pair_coeffs = lax.all_to_all(pair_send, 'lon', 0, 0, tiled=True)  50.6 us
    all_to_all x1, waiting for transfers between devices, shards(): lax.all_to_all(partial.astype(jnp.bfloat16).reshape(lon_count, 2 * wave_d...  44.7 us
    all_to_all x1, waiting for transfers between devices, shards(): lax.all_to_all(payload, 'lat', 0, 0, tiled=True).reshape(all_rows, -1)  39.3 us
    all_to_all x1, blocking collectives, shards(): lax.all_to_all(grad_units.reshape(lat_count, lat_rows, units_per_dev * un...  29.6 us
    all_to_all x1, starting transfers between devices, shards(): lax.all_to_all(partial.astype(jnp.bfloat16).reshape(lon_count, 2 * wave_d...  17.4 us
    all_to_all x1, blocking collectives, shards(): lax.all_to_all(half_send, 'lon', 0, 0, tiled=True, axis_index_groups=half...  15 us
    all_to_all x1, starting transfers between devices, shards(): lax.all_to_all(payload, 'lat', 0, 0, tiled=True).reshape(all_rows, -1)  8.19 us
  transfers between devices with their start and end apart: 3, of which 2 were waited for; matrix products, arithmetic and copies ran while one was open for 7% of the time, Pallas kernels for 0%

profile of v5, /device:TPU:32, one launch (start us, length us, event | category | flops | bytes accessed | tf_op | source)
XLA Modules:
  0.0 242.8 jit_solution(14513882978468961779)
XLA Ops:
  0.0 2.1 reshape.324
  2.1 1.4 copy.356
  3.5 4.5 %all-to-all-start = ((bf16[8,2,90,256]{3,1,2,0:T(2,128)(2,1)}), bf16[8,2,90,256]{3,1,2,0:T(2,128)(2,1)S(1)}, u32[]{:S(2)}, u32[]{:S(2)}) async-start(bf16[8,2,90,256]{3,1,2,0:T(2,128)(2,1)} %copy.356), calls=%async_computation | async-start | bytes 1474560 | tf_op jit(solution)/shard_map/all_to_all | solution.py:65
  8.0 1.2 fusion.19
  9.4 2.1 add_negate_fusion
  11.5 2.8 %neg.7 = f32[720,768]{1,0:T(8,128)} reshape(f32[8,90,768]{2,1,0:T(8,128)} %get-tuple-element.17) | data formatting | bytes 4423680 | tf_op jit(solution)/shard_map/neg | solution.py:28
  14.3 1.5 sub.77
  15.8 2.7 %fusion = (bf16[720,768]{1,0:T(8,128)(2,1)S(1)}, bf16[720,768]{1,0:T(8,128)(2,1)S(1)}) fusion(f32[720,768]{1,0:T(8,128)} %sub.77, f32[720,768]{1,0:T(8,128)} %neg.7, pred[768]{0:T(1024)(128)(4,1)S(1)} %fusion.73), kind=kLoop, calls=%fused_computation.4 | loop fusion | flops 3317760 | bytes 6636288 | tf_op jit(solution)/shard_map/convert_element_type | solution.py:30
  18.5 1.0 fusion.90
  19.6 0.6 copy.414
  20.3 0.6 copy.415
  20.9 0.6 copy.416
  21.5 0.6 copy.417
  22.1 0.8 fusion.7
  22.9 0.8 add_convert_fusion.1
  23.8 1.0 copy.359
  24.8 17.4 %all-to-all-start.1 = ((bf16[16,48,2,256]{3,1,2,0:T(8,128)(2,1)}), bf16[16,48,2,256]{3,1,2,0:T(8,128)(2,1)S(1)}, u32[]{:S(2)}, u32[]{:S(2)}) async-start(bf16[16,48,2,256]{3,1,2,0:T(8,128)(2,1)} %copy.359), calls=%async_computation.1 | async-start | bytes 1572864 | tf_op jit(solution)/shard_map/all_to_all | solution.py:70
  43.8 1.3 stack.131
  45.1 44.7 %all-to-all-done.1 = bf16[16,48,2,256]{3,1,2,0:T(8,128)(2,1)S(1)} async-done(((bf16[16,48,2,256]{3,1,2,0:T(8,128)(2,1)}), bf16[16,48,2,256]{3,1,2,0:T(8,128)(2,1)S(1)}, u32[]{:S(2)}, u32[]{:S(2)}) %all-to-all-start.1) | async-done | bytes 786464 | tf_op jit(solution)/shard_map/all_to_all | solution.py:70
  90.4 1.3 copy.418
  91.8 8.2 %all-to-all-start.2 = ((bf16[32,16,768]{2,1,0:T(8,128)(2,1)}), bf16[32,16,768]{2,1,0:T(8,128)(2,1)S(1)}, u32[]{:S(2)}, u32[]{:S(2)}) async-start(bf16[32,16,768]{2,1,0:T(8,128)(2,1)} %copy.418), calls=%async_computation.2 | async-start | bytes 1572864 | tf_op jit(solution)/shard_map/all_to_all | solution.py:84
  100.1 39.3 %all-to-all-done.2 = bf16[32,16,768]{2,1,0:T(8,128)(2,1)S(1)} async-done(((bf16[32,16,768]{2,1,0:T(8,128)(2,1)}), bf16[32,16,768]{2,1,0:T(8,128)(2,1)S(1)}, u32[]{:S(2)}, u32[]{:S(2)}) %all-to-all-start.2) | async-done | bytes 786464 | tf_op jit(solution)/shard_map/all_to_all | solution.py:84
  140.2 0.5 fusion.1
  140.7 0.5 fusion.25
  141.9 29.6 %all_to_all.30 = bf16[32,16,384]{2,1,0:T(8,128)(2,1)S(1)} all-to-all(bf16[32,16,384]{2,1,0:T(8,128)(2,1)S(1)} %convert_element_type.100), channel_id=1, replica_groups=mesh['lat'=32,'lon'=16] {'lat'}, dimensions={0} | all-to-all | bytes 786432 | tf_op jit(solution)/shard_map/all_to_all | solution.py:122
  172.0 50.6 %all_to_all.31 = bf16[16,2,48,256]{3,2,1,0:T(8,128)(2,1)S(1)} all-to-all(bf16[16,2,48,256]{3,2,1,0:T(8,128)(2,1)S(1)} %bitcast.171), channel_id=1, replica_groups=mesh['lat'=32,'lon'=16] {'lon'}, dimensions={0} | all-to-all | bytes 1572864 | tf_op jit(solution)/shard_map/all_to_all | solution.py:130
  222.6 0.7 fusion.5
  223.4 0.7 add_convert_fusion.2
  224.1 0.6 copy.427
  224.7 15.0 %all_to_all.32 = bf16[8,2,90,256]{3,1,2,0:T(2,128)(2,1)S(1)} all-to-all(bf16[8,2,90,256]{3,1,2,0:T(2,128)(2,1)S(1)} %bitcast.173), channel_id=1, replica_groups={{0,1,4,5,8,9,12,13},{2,3,6,7,10,11,14,15},{16,17,20,21,24,25,28,29},{18..., dimensions={0} | all-to-all | bytes 1474560 | tf_op jit(solution)/shard_map/all_to_all | solution.py:134
  240.3 0.7 copy-done.1
  241.5 1.3 copy.430
  (100 shorter events, 5.2 us)
Async XLA Ops:
  0.0 239.9 %copy-start = (bf16[256,256]{1,0:T(8,128)(2,1)S(1)}, bf16[256,256]{1,0:T(8,128)(2,1)}, u32[]{:S(2)}) copy-start(bf16[256,256]{1,0:T(8,128)(2,1)} %param.6) | copy-start | bytes 393220
  3.5 18.6 %all-to-all-start = ((bf16[8,2,90,256]{3,1,2,0:T(2,128)(2,1)}), bf16[8,2,90,256]{3,1,2,0:T(2,128)(2,1)S(1)}, u32[]{:S(2)}, u32[]{:S(2)}) async-start(bf16[8,2,90,256]{3,1,2,0:T(2,128)(2,1)} %copy.356), calls=%async_computation | async-start | bytes 1474560 | tf_op jit(solution)/shard_map/all_to_all | solution.py:65
  15.8 2.7 %copy-start.4 = (bf16[16,24,192]{2,1,0:T(8,128)(2,1)S(1)}, bf16[16,24,192]{2,1,0:T(8,128)(2,1)}, u32[]{:S(2)}) copy-start(bf16[16,24,192]{2,1,0:T(8,128)(2,1)} %param.5) | copy-start | bytes 442372
  18.5 4.4 %copy-start.2 = (bf16[720,768]{1,0:T(8,128)(2,1)}, bf16[720,768]{1,0:T(8,128)(2,1)S(1)}, u32[]{:S(2)}) copy-start(bf16[720,768]{1,0:T(8,128)(2,1)S(1)} %get-tuple-element.7) | copy-start | bytes 3317764
  24.7 18.5 %copy-start.10 = (bf16[16,1,192]{2,1,0:T(2,128)(2,1)S(1)}, bf16[16,1,192]{2,1,0:T(2,128)(2,1)}, u32[]{:S(2)}) copy-start(bf16[16,1,192]{2,1,0:T(2,128)(2,1)} %get-tuple-element.39) | copy-start | bytes 18436
  24.7 19.0 %copy-start.6 = (bf16[1,16,384]{2,0,1:T(2,128)(2,1)S(1)}, bf16[1,16,384]{2,0,1:T(2,128)(2,1)}, u32[]{:S(2)}) copy-start(bf16[1,16,384]{2,0,1:T(2,128)(2,1)} %copy.414) | copy-start | bytes 36868
  24.7 19.0 %copy-start.7 = (bf16[1,16,384]{2,0,1:T(2,128)(2,1)S(1)}, bf16[1,16,384]{2,0,1:T(2,128)(2,1)}, u32[]{:S(2)}) copy-start(bf16[1,16,384]{2,0,1:T(2,128)(2,1)} %copy.415) | copy-start | bytes 36868
  24.7 19.0 %copy-start.8 = (bf16[1,16,384]{2,0,1:T(2,128)(2,1)S(1)}, bf16[1,16,384]{2,0,1:T(2,128)(2,1)}, u32[]{:S(2)}) copy-start(bf16[1,16,384]{2,0,1:T(2,128)(2,1)} %copy.416) | copy-start | bytes 36868
  24.7 19.0 %copy-start.9 = (bf16[1,16,384]{2,0,1:T(2,128)(2,1)S(1)}, bf16[1,16,384]{2,0,1:T(2,128)(2,1)}, u32[]{:S(2)}) copy-start(bf16[1,16,384]{2,0,1:T(2,128)(2,1)} %copy.417) | copy-start | bytes 36868
  24.8 65.1 %all-to-all-start.1 = ((bf16[16,48,2,256]{3,1,2,0:T(8,128)(2,1)}), bf16[16,48,2,256]{3,1,2,0:T(8,128)(2,1)S(1)}, u32[]{:S(2)}, u32[]{:S(2)}) async-start(bf16[16,48,2,256]{3,1,2,0:T(8,128)(2,1)} %copy.359), calls=%async_computation.1 | async-start | bytes 1572864 | tf_op jit(solution)/shard_map/all_to_all | solution.py:70
  91.8 47.6 %all-to-all-start.2 = ((bf16[32,16,768]{2,1,0:T(8,128)(2,1)}), bf16[32,16,768]{2,1,0:T(8,128)(2,1)S(1)}, u32[]{:S(2)}, u32[]{:S(2)}) async-start(bf16[32,16,768]{2,1,0:T(8,128)(2,1)} %copy.418), calls=%async_computation.2 | async-start | bytes 1572864 | tf_op jit(solution)/shard_map/all_to_all | solution.py:84
  172.0 50.7 %copy-start.3 = (bf16[720,768]{1,0:T(8,128)(2,1)S(1)}, bf16[720,768]{1,0:T(8,128)(2,1)}, u32[]{:S(2)}) copy-start(bf16[720,768]{1,0:T(8,128)(2,1)} %copy-done.2) | copy-start | bytes 3317764
  239.9 1.1 copy-start.1
  239.9 1.1 copy-start.5

commit v6 on v3

--- a/solution.py
+++ b/solution.py
@@ -52,9 +52,9 @@
     half_groups = [lon_ids[:, h, :].reshape(-1).tolist() for h in range(halves)]
 
     pair_grid = lax.all_to_all(
-        cotangent.reshape(group, pair_rows, lon_dev, width), "lon", 0, 0, tiled=True,
+        cotangent.reshape(group, pair_rows * lon_dev, width), "lon", 0, 0, tiled=True,
         axis_index_groups=half_groups,
-    ).transpose(1, 0, 2, 3).reshape(pair_rows, group * lon_dev, width)
+    ).reshape(group, pair_rows, lon_dev, width).transpose(1, 0, 2, 3).reshape(pair_rows, group * lon_dev, width)
     partial = split_dot(table_hi, table_lo, pair_grid, (((0,), (1,)), ((), ())))
     partial_recv = lax.all_to_all(
         partial.astype(jnp.bfloat16).reshape(lon_count, 2 * wave_dev, pair_rows, width), "lon", 0, 0, tiled=True
@@ -120,6 +120,7 @@
     pair_coeffs = pair_coeffs.transpose(1, 0, 2, 3).reshape(pair_rows, 2 * wave_dev * lon_count, width)
     half_grid = split_dot(table_hi, table_lo, pair_coeffs, (((1,), (1,)), ((), ())))
     half_send = half_grid.astype(jnp.bfloat16).reshape(group, lon_dev, pair_rows, width).transpose(0, 2, 1, 3)
+    half_send = half_send.reshape(group, pair_rows * lon_dev, width)
     spatial = lax.all_to_all(
         half_send, "lon", 0, 0, tiled=True, axis_index_groups=half_groups
     ).reshape(lat_rows, lon_dev, width)

time: 243 us -> 241 us (level)
  transfers between devices with their start and end apart: 3 -> 3, of which waited for: 2 -> 3; matrix products, arithmetic and copies ran while one was open for 7% -> 6% of each run, Pallas kernels for 0% -> 0%
where the time goes in v6:
time: 241 us; the launch traced here: 240 us
  blocking collectives  95.4 us (40%)
  waiting for transfers between devices  85.4 us (35%)
  starting transfers between devices  28.8 us (12%)
  local copies, waits for them, and re-layouts  14 us (6%)
  other arithmetic  10.9 us (5%)
  matrix products  5.11 us (2%)
    all_to_all x1, blocking collectives, shards(): pair_coeffs = lax.all_to_all(pair_send, 'lon', 0, 0, tiled=True)  50.6 us
    all_to_all x1, waiting for transfers between devices, shards(): lax.all_to_all(partial.astype(jnp.bfloat16).reshape(lon_count, 2 * wave_d...  44.7 us
    all_to_all x1, waiting for transfers between devices, shards(): lax.all_to_all(payload, 'lat', 0, 0, tiled=True).reshape(all_rows, -1)  39.3 us
    all_to_all x1, blocking collectives, shards(): lax.all_to_all(grad_units.reshape(lat_count, lat_rows, units_per_dev * un...  29.6 us
    all_to_all x1, starting transfers between devices, shards(): lax.all_to_all(partial.astype(jnp.bfloat16).reshape(lon_count, 2 * wave_d...  16 us
    all_to_all x1, blocking collectives, shards(): lax.all_to_all(half_send, 'lon', 0, 0, tiled=True, axis_index_groups=half...  15.2 us
    convert_element_type x1, other arithmetic, fourier_table(): (table - high).astype(jnp.bfloat16)  9.52 us
    all_to_all x1, starting transfers between devices, shards(): lax.all_to_all(payload, 'lat', 0, 0, tiled=True).reshape(all_rows, -1)  8.19 us
  transfers between devices with their start and end apart: 3, of which 3 were waited for; matrix products, arithmetic and copies ran while one was open for 6% of the time, Pallas kernels for 0%

profile of v6, /device:TPU:32, one launch (start us, length us, event | category | flops | bytes accessed | tf_op | source)
XLA Modules:
  0.0 240.3 jit_solution(16884690322228764563)
XLA Ops:
  0.0 1.4 copy.369
  1.4 1.0 reshape.240
  2.4 4.6 %all-to-all-start = ((bf16[8,180,256]{2,1,0:T(8,128)(2,1)}), bf16[8,180,256]{2,1,0:T(8,128)(2,1)S(1)}, u32[]{:S(2)}, u32[]{:S(2)}) async-start(bf16[8,180,256]{2,1,0:T(8,128)(2,1)} %reshape.240), calls=%async_computation | async-start | bytes 1507328 | tf_op jit(solution)/shard_map/all_to_all | solution.py:54
  7.1 9.5 %fusion = (bf16[720,768]{1,0:T(8,128)(2,1)S(1)}, bf16[720,768]{1,0:T(8,128)(2,1)S(1)}) fusion(s32[768]{0:T(1024)S(1)} %get-tuple-element.100, s32[768]{0:T(1024)S(1)} %get-tuple-element.101, pred[768]{0:T(1024)(128)(4,1)S(1)} %get-tuple-element.103, s32[768]{0:T(1024)S(1)} %get-tuple-element.99, s32[768]{0:T(1024)S(1)} %get-tuple-element.102, ...), kind=kLoop, calls=%fused_computation.3 | loop fusion | flops 9953280 | bytes 2228544 | tf_op jit(solution)/shard_map/convert_element_type | solution.py:17
  16.6 1.0 fusion.95
  17.6 0.6 copy_bitcast_fusion.2
  18.4 1.4 all-to-all-done
  19.9 0.6 copy.371
  20.5 0.8 fusion.14
  21.3 0.8 add_convert_fusion.1
  22.2 1.0 copy.374
  23.2 16.0 %all-to-all-start.1 = ((bf16[16,48,2,256]{3,1,2,0:T(8,128)(2,1)}), bf16[16,48,2,256]{3,1,2,0:T(8,128)(2,1)S(1)}, u32[]{:S(2)}, u32[]{:S(2)}) async-start(bf16[16,48,2,256]{3,1,2,0:T(8,128)(2,1)} %copy.374), calls=%async_computation.1 | async-start | bytes 1572864 | tf_op jit(solution)/shard_map/all_to_all | solution.py:59
  40.9 1.3 stack.131
  42.2 44.7 %all-to-all-done.1 = bf16[16,48,2,256]{3,1,2,0:T(8,128)(2,1)S(1)} async-done(((bf16[16,48,2,256]{3,1,2,0:T(8,128)(2,1)}), bf16[16,48,2,256]{3,1,2,0:T(8,128)(2,1)S(1)}, u32[]{:S(2)}, u32[]{:S(2)}) %all-to-all-start.1) | async-done | bytes 786464 | tf_op jit(solution)/shard_map/all_to_all | solution.py:59
  86.9 0.2 reduce_sum.12
  87.5 1.3 copy.433
  88.8 8.2 %all-to-all-start.2 = ((bf16[32,16,768]{2,1,0:T(8,128)(2,1)}), bf16[32,16,768]{2,1,0:T(8,128)(2,1)S(1)}, u32[]{:S(2)}, u32[]{:S(2)}) async-start(bf16[32,16,768]{2,1,0:T(8,128)(2,1)} %copy.433), calls=%async_computation.2 | async-start | bytes 1572864 | tf_op jit(solution)/shard_map/all_to_all | solution.py:73
  97.1 39.3 %all-to-all-done.2 = bf16[32,16,768]{2,1,0:T(8,128)(2,1)S(1)} async-done(((bf16[32,16,768]{2,1,0:T(8,128)(2,1)}), bf16[32,16,768]{2,1,0:T(8,128)(2,1)S(1)}, u32[]{:S(2)}, u32[]{:S(2)}) %all-to-all-start.2) | async-done | bytes 786464 | tf_op jit(solution)/shard_map/all_to_all | solution.py:73
  137.2 0.5 fusion.8
  137.8 0.5 fusion.24
  138.3 0.3 copy.439
  138.7 0.3 convert_element_type.83
  139.0 29.6 %all_to_all.30 = bf16[32,16,384]{2,1,0:T(8,128)(2,1)S(1)} all-to-all(bf16[32,16,384]{2,1,0:T(8,128)(2,1)S(1)} %convert_element_type.83), channel_id=1, replica_groups=mesh['lat'=32,'lon'=16] {'lat'}, dimensions={0} | all-to-all | bytes 786432 | tf_op jit(solution)/shard_map/all_to_all | solution.py:111
  169.0 50.6 %all_to_all.31 = bf16[16,2,48,256]{3,2,1,0:T(8,128)(2,1)S(1)} all-to-all(bf16[16,2,48,256]{3,2,1,0:T(8,128)(2,1)S(1)} %bitcast.169), channel_id=1, replica_groups=mesh['lat'=32,'lon'=16] {'lon'}, dimensions={0} | all-to-all | bytes 1572864 | tf_op jit(solution)/shard_map/all_to_all | solution.py:119
  219.7 0.7 fusion.12
  220.4 0.7 add_convert_fusion.2
  221.2 0.6 copy.442
  222.0 15.2 %all_to_all.32 = bf16[8,180,256]{2,1,0:T(8,128)(2,1)S(1)} all-to-all(bf16[8,180,256]{2,1,0:T(8,128)(2,1)S(1)} %copy.444), channel_id=1, replica_groups={{0,1,4,5,8,9,12,13},{2,3,6,7,10,11,14,15},{16,17,20,21,24,25,28,29},{18..., dimensions={0} | all-to-all | bytes 1474560 | tf_op jit(solution)/shard_map/all_to_all | solution.py:124
  237.4 0.4 fusion.31
  237.8 0.7 copy-done.1
  238.5 0.5 add_convert_fusion
  239.0 1.3 copy.446
  (102 shorter events, 3.8 us)
Async XLA Ops:
  0.0 237.4 %copy-start = (bf16[256,256]{1,0:T(8,128)(2,1)S(1)}, bf16[256,256]{1,0:T(8,128)(2,1)}, u32[]{:S(2)}) copy-start(bf16[256,256]{1,0:T(8,128)(2,1)} %param.6) | copy-start | bytes 393220
  2.4 14.2 %copy-start.4 = (bf16[16,24,192]{2,1,0:T(8,128)(2,1)S(1)}, bf16[16,24,192]{2,1,0:T(8,128)(2,1)}, u32[]{:S(2)}) copy-start(bf16[16,24,192]{2,1,0:T(8,128)(2,1)} %param.5) | copy-start | bytes 442372
  2.4 17.4 %all-to-all-start = ((bf16[8,180,256]{2,1,0:T(8,128)(2,1)}), bf16[8,180,256]{2,1,0:T(8,128)(2,1)S(1)}, u32[]{:S(2)}, u32[]{:S(2)}) async-start(bf16[8,180,256]{2,1,0:T(8,128)(2,1)} %reshape.240), calls=%async_computation | async-start | bytes 1507328 | tf_op jit(solution)/shard_map/all_to_all | solution.py:54
  16.6 3.9 %copy-start.2 = (bf16[720,768]{1,0:T(8,128)(2,1)}, bf16[720,768]{1,0:T(8,128)(2,1)S(1)}, u32[]{:S(2)}) copy-start(bf16[720,768]{1,0:T(8,128)(2,1)S(1)} %get-tuple-element.7) | copy-start | bytes 3317764
  22.2 17.0 %copy-start.8 = (bf16[16,1,192]{2,1,0:T(2,128)(2,1)S(1)}, bf16[16,1,192]{2,1,0:T(2,128)(2,1)}, u32[]{:S(2)}) copy-start(bf16[16,1,192]{2,1,0:T(2,128)(2,1)} %get-tuple-element.21) | copy-start | bytes 18436
  22.2 17.0 %copy-start.9 = (bf16[16,1,192]{2,1,0:T(2,128)(2,1)S(1)}, bf16[16,1,192]{2,1,0:T(2,128)(2,1)}, u32[]{:S(2)}) copy-start(bf16[16,1,192]{2,1,0:T(2,128)(2,1)} %get-tuple-element.22) | copy-start | bytes 18436
  22.2 17.1 %copy-start.11 = (bf16[16,192]{1,0:T(8,128)(2,1)S(1)}, bf16[16,192]{1,0:T(8,128)(2,1)}, u32[]{:S(2)}) copy-start(bf16[16,192]{1,0:T(8,128)(2,1)} %get-tuple-element.84) | copy-start | bytes 18436
  22.2 17.3 %copy-start.6 = (bf16[16,1,192]{2,1,0:T(2,128)(2,1)S(1)}, bf16[16,1,192]{2,1,0:T(2,128)(2,1)}, u32[]{:S(2)}) copy-start(bf16[16,1,192]{2,1,0:T(2,128)(2,1)} %get-tuple-element.23) | copy-start | bytes 18436
  22.2 17.3 %copy-start.7 = (bf16[16,1,192]{2,1,0:T(2,128)(2,1)S(1)}, bf16[16,1,192]{2,1,0:T(2,128)(2,1)}, u32[]{:S(2)}) copy-start(bf16[16,1,192]{2,1,0:T(2,128)(2,1)} %get-tuple-element.24) | copy-start | bytes 18436
  23.2 17.1 %copy-start.10 = (bf16[16,1,192]{2,1,0:T(2,128)(2,1)S(1)}, bf16[16,1,192]{2,1,0:T(2,128)(2,1)}, u32[]{:S(2)}) copy-start(bf16[16,1,192]{2,1,0:T(2,128)(2,1)} %get-tuple-element.35) | copy-start | bytes 18436
  23.2 63.7 %all-to-all-start.1 = ((bf16[16,48,2,256]{3,1,2,0:T(8,128)(2,1)}), bf16[16,48,2,256]{3,1,2,0:T(8,128)(2,1)S(1)}, u32[]{:S(2)}, u32[]{:S(2)}) async-start(bf16[16,48,2,256]{3,1,2,0:T(8,128)(2,1)} %copy.374), calls=%async_computation.1 | async-start | bytes 1572864 | tf_op jit(solution)/shard_map/all_to_all | solution.py:59
  88.8 47.6 %all-to-all-start.2 = ((bf16[32,16,768]{2,1,0:T(8,128)(2,1)}), bf16[32,16,768]{2,1,0:T(8,128)(2,1)S(1)}, u32[]{:S(2)}, u32[]{:S(2)}) async-start(bf16[32,16,768]{2,1,0:T(8,128)(2,1)} %copy.433), calls=%async_computation.2 | async-start | bytes 1572864 | tf_op jit(solution)/shard_map/all_to_all | solution.py:73
  169.0 50.7 %copy-start.3 = (bf16[720,768]{1,0:T(8,128)(2,1)S(1)}, bf16[720,768]{1,0:T(8,128)(2,1)}, u32[]{:S(2)}) copy-start(bf16[720,768]{1,0:T(8,128)(2,1)} %copy-done.2) | copy-start | bytes 3317764
  237.4 1.1 copy-start.1
  237.4 1.1 copy-start.5

commit v7 on v6

--- a/solution.py
+++ b/solution.py
@@ -54,8 +54,11 @@
     pair_grid = lax.all_to_all(
         cotangent.reshape(group, pair_rows * lon_dev, width), "lon", 0, 0, tiled=True,
         axis_index_groups=half_groups,
-    ).reshape(group, pair_rows, lon_dev, width).transpose(1, 0, 2, 3).reshape(pair_rows, group * lon_dev, width)
-    partial = split_dot(table_hi, table_lo, pair_grid, (((0,), (1,)), ((), ())))
+    ).reshape(group, pair_rows, lon_dev, width)
+    partial = split_dot(
+        table_hi.reshape(group, lon_dev, -1), table_lo.reshape(group, lon_dev, -1), pair_grid,
+        (((0, 1), (0, 2)), ((), ())),
+    )
     partial_recv = lax.all_to_all(
         partial.astype(jnp.bfloat16).reshape(lon_count, 2 * wave_dev, pair_rows, width), "lon", 0, 0, tiled=True
     ).reshape(lon_count // 4, halves, 2, 2 * wave_dev, pair_rows, width)

time: 241 us -> 253 us (1.050)
  local copies, waits for them, and re-layouts: 14 us -> 34.6 us
  waiting for transfers between devices: 85.4 us -> 66.6 us
  matrix products: 5.11 us -> 9.98 us
  other arithmetic: 10.9 us -> 14.3 us
    all_to_all x1, waiting for transfers between devices: 44.7 us -> 27.3 us  [shards(): lax.all_to_all(partial.astype(jnp.bfloat16).reshape(lon_count, 2 * wave_d...]
    another operation x33, local copies, waits for them, and re-layouts: 1.99 us -> 15.2 us  [shards(): jnp.stack([jnp.concatenate([legendre[:, a], legendre[:, b]], axis=-1) for...]
    squeeze x8, local copies, waits for them, and re-layouts: 0.05 us -> 2.99 us  [shards(): legendre[:, b]]
  transfers between devices with their start and end apart: 3 -> 3, of which waited for: 3 -> 2; matrix products, arithmetic and copies ran while one was open for 6% -> 13% of each run, Pallas kernels for 0% -> 0%
where the time goes in v7:
time: 253 us; the launch traced here: 251 us
  blocking collectives  95.3 us (38%)
  waiting for transfers between devices  66.6 us (26%)
  local copies, waits for them, and re-layouts  34.6 us (14%)
  starting transfers between devices  30 us (12%)
  other arithmetic  14.3 us (6%)
  matrix products  9.98 us (4%)
    all_to_all x1, blocking collectives, shards(): pair_coeffs = lax.all_to_all(pair_send, 'lon', 0, 0, tiled=True)  50.5 us
    all_to_all x1, waiting for transfers between devices, shards(): lax.all_to_all(payload, 'lat', 0, 0, tiled=True).reshape(all_rows, -1)  39.3 us
    all_to_all x1, blocking collectives, shards(): lax.all_to_all(grad_units.reshape(lat_count, lat_rows, units_per_dev * un...  29.6 us
    all_to_all x1, waiting for transfers between devices, shards(): lax.all_to_all(partial.astype(jnp.bfloat16).reshape(lon_count, 2 * wave_d...  27.3 us
    all_to_all x1, starting transfers between devices, shards(): lax.all_to_all(partial.astype(jnp.bfloat16).reshape(lon_count, 2 * wave_d...  17.2 us
    another operation x33, local copies, waits for them, and re-layouts, shards(): jnp.stack([jnp.concatenate([legendre[:, a], legendre[:, b]], axis=-1) for...  15.2 us
    all_to_all x1, blocking collectives, shards(): lax.all_to_all(half_send, 'lon', 0, 0, tiled=True, axis_index_groups=half...  15.2 us
    convert_element_type x1, other arithmetic, fourier_table(): (table - high).astype(jnp.bfloat16)  9.52 us
  transfers between devices with their start and end apart: 3, of which 2 were waited for; matrix products, arithmetic and copies ran while one was open for 13% of the time, Pallas kernels for 0%

profile of v7, /device:TPU:32, one launch (start us, length us, event | category | flops | bytes accessed | tf_op | source)
XLA Modules:
  0.0 251.3 jit_solution(8404129330440150727)
XLA Ops:
  0.0 1.4 copy.364
  1.4 1.0 reshape.244
  2.4 4.6 %all-to-all-start = ((bf16[8,180,256]{2,1,0:T(8,128)(2,1)}), bf16[8,180,256]{2,1,0:T(8,128)(2,1)S(1)}, u32[]{:S(2)}, u32[]{:S(2)}) async-start(bf16[8,180,256]{2,1,0:T(8,128)(2,1)} %reshape.244), calls=%async_computation | async-start | bytes 1507328 | tf_op jit(solution)/shard_map/all_to_all | solution.py:54
  7.1 9.5 %fusion = (bf16[720,768]{1,0:T(8,128)(2,1)S(1)}, bf16[720,768]{1,0:T(8,128)(2,1)S(1)}) fusion(s32[768]{0:T(1024)S(1)} %get-tuple-element.100, s32[768]{0:T(1024)S(1)} %get-tuple-element.101, pred[768]{0:T(1024)(128)(4,1)S(1)} %get-tuple-element.103, s32[768]{0:T(1024)S(1)} %get-tuple-element.99, s32[768]{0:T(1024)S(1)} %get-tuple-element.102, ...), kind=kLoop, calls=%fused_computation.3 | loop fusion | flops 9953280 | bytes 2228544 | tf_op jit(solution)/shard_map/convert_element_type | solution.py:17
  16.6 0.9 fusion.94
  17.6 1.2 reshape.256
  18.8 1.2 reshape.258
  20.3 2.2 fusion.15
  22.5 0.8 fusion.8
  23.3 1.0 copy.368
  24.3 17.2 %all-to-all-start.1 = ((bf16[16,48,2,256]{3,1,2,0:T(8,128)(2,1)}), bf16[16,48,2,256]{3,1,2,0:T(8,128)(2,1)S(1)}, u32[]{:S(2)}, u32[]{:S(2)}) async-start(bf16[16,48,2,256]{3,1,2,0:T(8,128)(2,1)} %copy.368), calls=%async_computation.1 | async-start | bytes 1572864 | tf_op jit(solution)/shard_map/all_to_all | solution.py:62
  41.7 0.7 copy_bitcast_fusion.6
  44.5 0.7 copy_bitcast_fusion.10
  47.8 0.7 copy_bitcast_fusion.12
  48.6 0.7 copy_bitcast_fusion.14
  56.5 5.5 %stack.131 = bf16[32,16,384]{2,0,1:T(8,128)(2,1)} concatenate(bf16[1,16,384]{2,0,1:T(2,128)(2,1)S(1)} %copy.395, bf16[1,16,384]{2,0,1:T(2,128)(2,1)S(1)} %copy.396, bf16[1,16,384]{2,0,1:T(2,128)(2,1)S(1)} %copy.397, bf16[1,16,384]{2,0,1:T(2,128)(2,1)S(1)} %copy.398, bf16[1,16,384]{2,0,1:T(2,128)(2,1)S(1)} %copy.399, bf16[1,16,384]{2,0,1:T(2,128)(2,1)S(1)} %copy.400, ...), dimensions={0} | concatenate | bytes 786432 | tf_op jit(solution)/shard_map/stack | solution.py:72
  61.9 27.3 %all-to-all-done.1 = bf16[16,48,2,256]{3,1,2,0:T(8,128)(2,1)S(1)} async-done(((bf16[16,48,2,256]{3,1,2,0:T(8,128)(2,1)}), bf16[16,48,2,256]{3,1,2,0:T(8,128)(2,1)S(1)}, u32[]{:S(2)}, u32[]{:S(2)}) %all-to-all-start.1) | async-done | bytes 786464 | tf_op jit(solution)/shard_map/all_to_all | solution.py:62
  89.7 1.1 pad_maximum_fusion
  90.8 1.3 copy.427
  92.1 8.2 %all-to-all-start.2 = ((bf16[32,16,768]{2,1,0:T(8,128)(2,1)}), bf16[32,16,768]{2,1,0:T(8,128)(2,1)S(1)}, u32[]{:S(2)}, u32[]{:S(2)}) async-start(bf16[32,16,768]{2,1,0:T(8,128)(2,1)} %copy.427), calls=%async_computation.2 | async-start | bytes 1572864 | tf_op jit(solution)/shard_map/all_to_all | solution.py:76
  100.5 39.3 %all-to-all-done.2 = bf16[32,16,768]{2,1,0:T(8,128)(2,1)S(1)} async-done(((bf16[32,16,768]{2,1,0:T(8,128)(2,1)}), bf16[32,16,768]{2,1,0:T(8,128)(2,1)S(1)}, u32[]{:S(2)}, u32[]{:S(2)}) %all-to-all-start.2) | async-done | bytes 786464 | tf_op jit(solution)/shard_map/all_to_all | solution.py:76
  139.8 0.8 fusion.18
  140.8 1.1 copy.431
  141.9 1.1 copy.429
  143.0 0.9 broadcast_select_fusion
  143.9 2.4 fusion.9
  146.3 2.2 fusion.23
  148.5 1.0 pad_maximum_fusion.1
  150.1 29.6 %all_to_all.30 = bf16[32,16,384]{2,1,0:T(8,128)(2,1)S(1)} all-to-all(bf16[32,16,384]{2,1,0:T(8,128)(2,1)S(1)} %convert_element_type.83), channel_id=1, replica_groups=mesh['lat'=32,'lon'=16] {'lat'}, dimensions={0} | all-to-all | bytes 786432 | tf_op jit(solution)/shard_map/all_to_all | solution.py:114
  180.2 50.5 %all_to_all.31 = bf16[16,2,48,256]{3,2,1,0:T(8,128)(2,1)S(1)} all-to-all(bf16[16,2,48,256]{3,2,1,0:T(8,128)(2,1)S(1)} %bitcast.172), channel_id=1, replica_groups=mesh['lat'=32,'lon'=16] {'lon'}, dimensions={0} | all-to-all | bytes 1572864 | tf_op jit(solution)/shard_map/all_to_all | solution.py:122
  233.0 15.2 %all_to_all.32 = bf16[8,180,256]{2,1,0:T(8,128)(2,1)S(1)} all-to-all(bf16[8,180,256]{2,1,0:T(8,128)(2,1)S(1)} %copy.438), channel_id=1, replica_groups={{0,1,4,5,8,9,12,13},{2,3,6,7,10,11,14,15},{16,17,20,21,24,25,28,29},{18..., dimensions={0} | all-to-all | bytes 1474560 | tf_op jit(solution)/shard_map/all_to_all | solution.py:127
  250.0 1.3 copy.440
  (91 shorter events, 18.2 us)
Async XLA Ops:
  0.0 248.4 %copy-start = (bf16[256,256]{1,0:T(8,128)(2,1)S(1)}, bf16[256,256]{1,0:T(8,128)(2,1)}, u32[]{:S(2)}) copy-start(bf16[256,256]{1,0:T(8,128)(2,1)} %param.6) | copy-start | bytes 393220
  2.4 14.2 %copy-start.3 = (bf16[16,24,192]{2,1,0:T(8,128)(2,1)S(1)}, bf16[16,24,192]{2,1,0:T(8,128)(2,1)}, u32[]{:S(2)}) copy-start(bf16[16,24,192]{2,1,0:T(8,128)(2,1)} %param.5) | copy-start | bytes 442372
  2.4 17.7 %all-to-all-start = ((bf16[8,180,256]{2,1,0:T(8,128)(2,1)}), bf16[8,180,256]{2,1,0:T(8,128)(2,1)S(1)}, u32[]{:S(2)}, u32[]{:S(2)}) async-start(bf16[8,180,256]{2,1,0:T(8,128)(2,1)} %reshape.244), calls=%async_computation | async-start | bytes 1507328 | tf_op jit(solution)/shard_map/all_to_all | solution.py:54
  20.3 2.2 copy-start.2
  24.3 64.9 %all-to-all-start.1 = ((bf16[16,48,2,256]{3,1,2,0:T(8,128)(2,1)}), bf16[16,48,2,256]{3,1,2,0:T(8,128)(2,1)S(1)}, u32[]{:S(2)}, u32[]{:S(2)}) async-start(bf16[16,48,2,256]{3,1,2,0:T(8,128)(2,1)} %copy.368), calls=%async_computation.1 | async-start | bytes 1572864 | tf_op jit(solution)/shard_map/all_to_all | solution.py:62
  92.1 47.6 %all-to-all-start.2 = ((bf16[32,16,768]{2,1,0:T(8,128)(2,1)}), bf16[32,16,768]{2,1,0:T(8,128)(2,1)S(1)}, u32[]{:S(2)}, u32[]{:S(2)}) async-start(bf16[32,16,768]{2,1,0:T(8,128)(2,1)} %copy.427), calls=%async_computation.2 | async-start | bytes 1572864 | tf_op jit(solution)/shard_map/all_to_all | solution.py:76
  143.9 2.4 copy-start.4
  248.4 1.1 copy-start.1
  248.4 1.1 copy-start.5

commit v8 on v6

--- a/solution.py
+++ b/solution.py
@@ -13,13 +13,11 @@
     phases = (longitude[:, None] * (column // 2) + (count_lon // 4) * (column % 2)) % count_lon
     angles = phases.astype(jnp.float32) * (2.0 * math.pi / count_lon)
     table = math.sqrt(2.0 / count_lon) * jnp.cos(angles)
-    high = lax.reduce_precision(table, exponent_bits=8, mantissa_bits=7)
-    return lax.optimization_barrier((high.astype(jnp.bfloat16), (table - high).astype(jnp.bfloat16)))
+    return lax.optimization_barrier(table.astype(jnp.bfloat16))
 
 
-def split_dot(table_hi, table_lo, values, dims):
-    dot = lambda t: lax.dot_general(t, values, dims, preferred_element_type=jnp.float32)
-    return dot(table_hi) + dot(table_lo)
+def table_dot(table, values, dims):
+    return lax.dot_general(table, values, dims, preferred_element_type=jnp.float32)
 
 
 def unit_slots(lat_count, units_per_dev):
@@ -47,7 +45,7 @@
     longitude = lon_dev * ((position // 2) * 4 + 2 * own_half + position % 2) + jnp.arange(
         group * lon_dev
     ) % lon_dev
-    table_hi, table_lo = fourier_table(longitude, count_lon, wave_dev * lon_count)
+    table = fourier_table(longitude, count_lon, wave_dev * lon_count)
     lon_ids = np.arange(lon_count).reshape(lon_count // 4, halves, 2)
     half_groups = [lon_ids[:, h, :].reshape(-1).tolist() for h in range(halves)]
 
@@ -55,7 +53,7 @@
         cotangent.reshape(group, pair_rows * lon_dev, width), "lon", 0, 0, tiled=True,
         axis_index_groups=half_groups,
     ).reshape(group, pair_rows, lon_dev, width).transpose(1, 0, 2, 3).reshape(pair_rows, group * lon_dev, width)
-    partial = split_dot(table_hi, table_lo, pair_grid, (((0,), (1,)), ((), ())))
+    partial = table_dot(table, pair_grid, (((0,), (1,)), ((), ())))
     partial_recv = lax.all_to_all(
         partial.astype(jnp.bfloat16).reshape(lon_count, 2 * wave_dev, pair_rows, width), "lon", 0, 0, tiled=True
     ).reshape(lon_count // 4, halves, 2, 2 * wave_dev, pair_rows, width)
@@ -118,7 +116,7 @@
     ).reshape(lon_count, pair_rows, 2 * wave_dev, width)
     pair_coeffs = lax.all_to_all(pair_send, "lon", 0, 0, tiled=True)
     pair_coeffs = pair_coeffs.transpose(1, 0, 2, 3).reshape(pair_rows, 2 * wave_dev * lon_count, width)
-    half_grid = split_dot(table_hi, table_lo, pair_coeffs, (((1,), (1,)), ((), ())))
+    half_grid = table_dot(table, pair_coeffs, (((1,), (1,)), ((), ())))
     half_send = half_grid.astype(jnp.bfloat16).reshape(group, lon_dev, pair_rows, width).transpose(0, 2, 1, 3)
     half_send = half_send.reshape(group, pair_rows * lon_dev, width)
     spatial = lax.all_to_all(

time: 241 us -> 238 us (0.988)
  transfers between devices with their start and end apart: 3 -> 3, of which waited for: 3 -> 3; matrix products, arithmetic and copies ran while one was open for 6% -> 5% of each run, Pallas kernels for 0% -> 0%
where the time goes in v8:
time: 238 us; the launch traced here: 237 us
  blocking collectives  95.3 us (40%)
  waiting for transfers between devices  86.9 us (37%)
  starting transfers between devices  27.7 us (12%)
  local copies, waits for them, and re-layouts  12.7 us (5%)
  other arithmetic  10.6 us (4%)
  matrix products  3.57 us (2%)
    all_to_all x1, blocking collectives, shards(): pair_coeffs = lax.all_to_all(pair_send, 'lon', 0, 0, tiled=True)  50.5 us
    all_to_all x1, waiting for transfers between devices, shards(): lax.all_to_all(partial.astype(jnp.bfloat16).reshape(lon_count, 2 * wave_d...  44.8 us
    all_to_all x1, waiting for transfers between devices, shards(): lax.all_to_all(payload, 'lat', 0, 0, tiled=True).reshape(all_rows, -1)  39.3 us
    all_to_all x1, blocking collectives, shards(): lax.all_to_all(grad_units.reshape(lat_count, lat_rows, units_per_dev * un...  29.6 us
    all_to_all x1, blocking collectives, shards(): lax.all_to_all(half_send, 'lon', 0, 0, tiled=True, axis_index_groups=half...  15.2 us
    all_to_all x1, starting transfers between devices, shards(): lax.all_to_all(partial.astype(jnp.bfloat16).reshape(lon_count, 2 * wave_d...  14.9 us
    convert_element_type x1, other arithmetic, fourier_table(): return lax.optimization_barrier(table.astype(jnp.bfloat16))  9.23 us
    all_to_all x1, starting transfers between devices, shards(): lax.all_to_all(payload, 'lat', 0, 0, tiled=True).reshape(all_rows, -1)  8.2 us
  transfers between devices with their start and end apart: 3, of which 3 were waited for; matrix products, arithmetic and copies ran while one was open for 5% of the time, Pallas kernels for 0%

profile of v8, /device:TPU:32, one launch (start us, length us, event | category | flops | bytes accessed | tf_op | source)
XLA Modules:
  0.0 237.4 jit_solution(10564786186344363198)
XLA Ops:
  0.0 1.4 copy.364
  1.4 1.0 reshape.240
  2.4 4.6 %all-to-all-start = ((bf16[8,180,256]{2,1,0:T(8,128)(2,1)}), bf16[8,180,256]{2,1,0:T(8,128)(2,1)S(1)}, u32[]{:S(2)}, u32[]{:S(2)}) async-start(bf16[8,180,256]{2,1,0:T(8,128)(2,1)} %reshape.240), calls=%async_computation | async-start | bytes 1507328 | tf_op jit(solution)/shard_map/all_to_all | solution.py:52
  7.1 9.2 %fusion.4 = bf16[720,768]{1,0:T(8,128)(2,1)S(1)} fusion(s32[768]{0:T(1024)S(1)} %get-tuple-element.94, s32[768]{0:T(1024)S(1)} %get-tuple-element.95, s32[768]{0:T(1024)S(1)} %get-tuple-element.93, s32[768]{0:T(1024)S(1)} %get-tuple-element.96, s32[720]{0:T(1024)S(1)} %fusion.75, pred[768]{0:T(1024)(128)(4,1)S(1)} %get-tuple-element.97, ...), kind=kLoop, calls=%fused_computation.5 | loop fusion | flops 8294400 | bytes 1122624 | tf_op jit(solution)/shard_map/convert_element_type | solution.py:16
  16.3 0.3 fusion.90
  16.9 2.9 %all-to-all-done = bf16[8,180,256]{2,1,0:T(8,128)(2,1)S(1)} async-done(((bf16[8,180,256]{2,1,0:T(8,128)(2,1)}), bf16[8,180,256]{2,1,0:T(8,128)(2,1)S(1)}, u32[]{:S(2)}, u32[]{:S(2)}) %all-to-all-start) | async-done | bytes 737312 | tf_op jit(solution)/shard_map/all_to_all | solution.py:52
  19.9 0.6 copy.366
  20.5 0.8 convolution_convert_fusion
  21.3 1.0 copy.368
  22.3 14.9 %all-to-all-start.1 = ((bf16[16,48,2,256]{3,1,2,0:T(8,128)(2,1)}), bf16[16,48,2,256]{3,1,2,0:T(8,128)(2,1)S(1)}, u32[]{:S(2)}, u32[]{:S(2)}) async-start(bf16[16,48,2,256]{3,1,2,0:T(8,128)(2,1)} %copy.368), calls=%async_computation.1 | async-start | bytes 1572864 | tf_op jit(solution)/shard_map/all_to_all | solution.py:57
  38.8 1.3 stack.131
  40.1 44.8 %all-to-all-done.1 = bf16[16,48,2,256]{3,1,2,0:T(8,128)(2,1)S(1)} async-done(((bf16[16,48,2,256]{3,1,2,0:T(8,128)(2,1)}), bf16[16,48,2,256]{3,1,2,0:T(8,128)(2,1)S(1)}, u32[]{:S(2)}, u32[]{:S(2)}) %all-to-all-start.1) | async-done | bytes 786464 | tf_op jit(solution)/shard_map/all_to_all | solution.py:57
  84.9 0.2 reduce_sum.12
  85.1 0.2 reshape_reshape.4
  85.5 1.3 copy.427
  86.8 8.2 %all-to-all-start.2 = ((bf16[32,16,768]{2,1,0:T(8,128)(2,1)}), bf16[32,16,768]{2,1,0:T(8,128)(2,1)S(1)}, u32[]{:S(2)}, u32[]{:S(2)}) async-start(bf16[32,16,768]{2,1,0:T(8,128)(2,1)} %copy.427), calls=%async_computation.2 | async-start | bytes 1572864 | tf_op jit(solution)/shard_map/all_to_all | solution.py:71
  95.1 39.3 %all-to-all-done.2 = bf16[32,16,768]{2,1,0:T(8,128)(2,1)S(1)} async-done(((bf16[32,16,768]{2,1,0:T(8,128)(2,1)}), bf16[32,16,768]{2,1,0:T(8,128)(2,1)S(1)}, u32[]{:S(2)}, u32[]{:S(2)}) %all-to-all-start.2) | async-done | bytes 786464 | tf_op jit(solution)/shard_map/all_to_all | solution.py:71
  134.5 0.2 copy.428
  135.2 0.5 fusion.8
  135.7 0.5 fusion.19
  136.3 0.3 copy.433
  136.7 0.3 convert_element_type.79
  137.0 29.6 %all_to_all.30 = bf16[32,16,384]{2,1,0:T(8,128)(2,1)S(1)} all-to-all(bf16[32,16,384]{2,1,0:T(8,128)(2,1)S(1)} %convert_element_type.79), channel_id=1, replica_groups=mesh['lat'=32,'lon'=16] {'lat'}, dimensions={0} | all-to-all | bytes 786432 | tf_op jit(solution)/shard_map/all_to_all | solution.py:109
  166.7 0.2 broadcast_in_dim.65
  167.0 50.5 %all_to_all.31 = bf16[16,2,48,256]{3,2,1,0:T(8,128)(2,1)S(1)} all-to-all(bf16[16,2,48,256]{3,2,1,0:T(8,128)(2,1)S(1)} %bitcast.163), channel_id=1, replica_groups=mesh['lat'=32,'lon'=16] {'lon'}, dimensions={0} | all-to-all | bytes 1572864 | tf_op jit(solution)/shard_map/all_to_all | solution.py:117
  217.5 0.7 convolution_convert_fusion.1
  218.3 0.6 copy.436
  219.1 15.2 %all_to_all.32 = bf16[8,180,256]{2,1,0:T(8,128)(2,1)S(1)} all-to-all(bf16[8,180,256]{2,1,0:T(8,128)(2,1)S(1)} %copy.438), channel_id=1, replica_groups={{0,1,4,5,8,9,12,13},{2,3,6,7,10,11,14,15},{16,17,20,21,24,25,28,29},{18..., dimensions={0} | all-to-all | bytes 1474560 | tf_op jit(solution)/shard_map/all_to_all | solution.py:122
  234.5 0.4 fusion.26
  234.9 0.7 copy-done.1
  235.6 0.5 add_convert_fusion
  236.1 1.3 copy.440
  (84 shorter events, 3.0 us)
Async XLA Ops:
  0.0 234.5 %copy-start = (bf16[256,256]{1,0:T(8,128)(2,1)S(1)}, bf16[256,256]{1,0:T(8,128)(2,1)}, u32[]{:S(2)}) copy-start(bf16[256,256]{1,0:T(8,128)(2,1)} %param.6) | copy-start | bytes 393220
  2.4 13.9 %copy-start.2 = (bf16[16,24,192]{2,1,0:T(8,128)(2,1)S(1)}, bf16[16,24,192]{2,1,0:T(8,128)(2,1)}, u32[]{:S(2)}) copy-start(bf16[16,24,192]{2,1,0:T(8,128)(2,1)} %param.5) | copy-start | bytes 442372
  2.4 17.4 %all-to-all-start = ((bf16[8,180,256]{2,1,0:T(8,128)(2,1)}), bf16[8,180,256]{2,1,0:T(8,128)(2,1)S(1)}, u32[]{:S(2)}, u32[]{:S(2)}) async-start(bf16[8,180,256]{2,1,0:T(8,128)(2,1)} %reshape.240), calls=%async_computation | async-start | bytes 1507328 | tf_op jit(solution)/shard_map/all_to_all | solution.py:52
  22.3 62.6 %all-to-all-start.1 = ((bf16[16,48,2,256]{3,1,2,0:T(8,128)(2,1)}), bf16[16,48,2,256]{3,1,2,0:T(8,128)(2,1)S(1)}, u32[]{:S(2)}, u32[]{:S(2)}) async-start(bf16[16,48,2,256]{3,1,2,0:T(8,128)(2,1)} %copy.368), calls=%async_computation.1 | async-start | bytes 1572864 | tf_op jit(solution)/shard_map/all_to_all | solution.py:57
  86.8 47.6 %all-to-all-start.2 = ((bf16[32,16,768]{2,1,0:T(8,128)(2,1)}), bf16[32,16,768]{2,1,0:T(8,128)(2,1)S(1)}, u32[]{:S(2)}, u32[]{:S(2)}) async-start(bf16[32,16,768]{2,1,0:T(8,128)(2,1)} %copy.427), calls=%async_computation.2 | async-start | bytes 1572864 | tf_op jit(solution)/shard_map/all_to_all | solution.py:71
  234.5 1.1 copy-start.1
  234.5 1.1 copy-start.3

commit v9 on v8

--- a/solution.py
+++ b/solution.py
@@ -57,12 +57,14 @@
     partial_recv = lax.all_to_all(
         partial.astype(jnp.bfloat16).reshape(lon_count, 2 * wave_dev, pair_rows, width), "lon", 0, 0, tiled=True
     ).reshape(lon_count // 4, halves, 2, 2 * wave_dev, pair_rows, width)
-    coeffs = jnp.sum(partial_recv.astype(jnp.float32), axis=1).astype(jnp.bfloat16)
-    coeffs = coeffs.transpose(0, 1, 3, 2, 4).reshape(lat_rows, 2 * wave_dev, width)
     units_total = wave_dev * 4
     units_per_dev = units_total // lat_count
     unit_width = width // 2
-    unit_send = coeffs.reshape(lat_rows, lat_count, units_per_dev * unit_width).transpose(1, 0, 2)
+    summed = jnp.sum(partial_recv.astype(jnp.float32), axis=1).astype(jnp.bfloat16)
+    summed = summed.reshape(lon_count // 4, 2, 2 * wave_dev, pair_rows, 2, unit_width)
+    unit_send = summed.transpose(2, 4, 0, 1, 3, 5).reshape(
+        lat_count, units_per_dev, lat_rows, unit_width
+    ).transpose(0, 2, 1, 3).reshape(lat_count, lat_rows, units_per_dev * unit_width)
     slots = unit_slots(lat_count, units_per_dev)
     basis_send = jnp.stack(
         [jnp.concatenate([legendre[:, a], legendre[:, b]], axis=-1) for a, b in slots.tolist()]

time: 238 us -> 238 us (level)
  local copies, waits for them, and re-layouts: 12.7 us -> 9.66 us
  other arithmetic: 10.6 us -> 13.5 us
    unnamed x0 -> x31, other arithmetic: none -> 2.56 us
where the time goes in v9:
time: 238 us
  blocking collectives  95.3 us (40%)
  waiting for transfers between devices  87.2 us (37%)
  starting transfers between devices  28.2 us (12%)
  other arithmetic  13.5 us (6%)
  local copies, waits for them, and re-layouts  9.66 us (4%)
  matrix products  3.56 us (1%)
    all_to_all x1, blocking collectives, shards(): pair_coeffs = lax.all_to_all(pair_send, 'lon', 0, 0, tiled=True)  50.4 us
    all_to_all x1, waiting for transfers between devices, shards(): lax.all_to_all(partial.astype(jnp.bfloat16).reshape(lon_count, 2 * wave_d...  46.2 us
    all_to_all x1, waiting for transfers between devices, shards(): lax.all_to_all(payload, 'lat', 0, 0, tiled=True).reshape(all_rows, -1)  39.3 us
    all_to_all x1, blocking collectives, shards(): lax.all_to_all(grad_units.reshape(lat_count, lat_rows, units_per_dev * un...  29.6 us
    all_to_all x1, starting transfers between devices, shards(): lax.all_to_all(partial.astype(jnp.bfloat16).reshape(lon_count, 2 * wave_d...  15.5 us
    all_to_all x1, blocking collectives, shards(): lax.all_to_all(half_send, 'lon', 0, 0, tiled=True, axis_index_groups=half...  15.2 us
    convert_element_type x1, other arithmetic, fourier_table(): return lax.optimization_barrier(table.astype(jnp.bfloat16))  9.23 us
    all_to_all x1, starting transfers between devices, shards(): lax.all_to_all(payload, 'lat', 0, 0, tiled=True).reshape(all_rows, -1)  8.18 us
  transfers between devices with their start and end apart: 3, of which 3 were waited for; matrix products, arithmetic and copies ran while one was open for 5% of the time, Pallas kernels for 0%

profile of v9, /device:TPU:32, one launch (start us, length us, event | category | flops | bytes accessed | tf_op | source)
XLA Modules:
  0.0 237.8 jit_solution(4858278054150878008)
XLA Ops:
  0.0 1.4 copy.115
  1.4 1.0 reshape.249
  2.4 4.5 %all-to-all-start = ((bf16[8,180,256]{2,1,0:T(8,128)(2,1)}), bf16[8,180,256]{2,1,0:T(8,128)(2,1)S(1)}, u32[]{:S(2)}, u32[]{:S(2)}) async-start(bf16[8,180,256]{2,1,0:T(8,128)(2,1)} %reshape.249), calls=%async_computation | async-start | bytes 1507328 | tf_op jit(solution)/shard_map/all_to_all | solution.py:52
  7.0 0.3 fusion.91
  8.4 9.2 %fusion.4 = bf16[720,768]{1,0:T(8,128)(2,1)S(1)} fusion(s32[768]{0:T(1024)S(1)} %get-tuple-element.64, s32[768]{0:T(1024)S(1)} %get-tuple-element.65, s32[768]{0:T(1024)S(1)} %get-tuple-element.63, s32[768]{0:T(1024)S(1)} %get-tuple-element.66, s32[720]{0:T(1024)S(1)} %fusion.75, pred[768]{0:T(1024)(128)(4,1)S(1)} %get-tuple-element.67, ...), kind=kLoop, calls=%fused_computation.5 | loop fusion | flops 8294400 | bytes 1122624 | tf_op jit(solution)/shard_map/convert_element_type | solution.py:16
  17.9 1.7 all-to-all-done
  19.8 0.6 copy.117
  20.4 0.8 convolution_convert_fusion
  21.2 1.0 copy.119
  22.2 15.5 %all-to-all-start.1 = ((bf16[16,48,2,256]{3,1,2,0:T(8,128)(2,1)}), bf16[16,48,2,256]{3,1,2,0:T(8,128)(2,1)S(1)}, u32[]{:S(2)}, u32[]{:S(2)}) async-start(bf16[16,48,2,256]{3,1,2,0:T(8,128)(2,1)} %copy.119), calls=%async_computation.1 | async-start | bytes 1572864 | tf_op jit(solution)/shard_map/all_to_all | solution.py:57
  39.2 46.2 %all-to-all-done.1 = bf16[16,48,2,256]{3,1,2,0:T(8,128)(2,1)S(1)} async-done(((bf16[16,48,2,256]{3,1,2,0:T(8,128)(2,1)}), bf16[16,48,2,256]{3,1,2,0:T(8,128)(2,1)S(1)}, u32[]{:S(2)}, u32[]{:S(2)}) %all-to-all-start.1) | async-done | bytes 786464 | tf_op jit(solution)/shard_map/all_to_all | solution.py:57
  85.4 0.2 reduce_sum.12
  85.8 0.3 copy.122
  86.2 1.0 pad_maximum_fusion
  87.2 8.2 %all-to-all-start.2 = ((bf16[32,16,768]{2,1,0:T(8,128)(2,1)}), bf16[32,16,768]{2,1,0:T(8,128)(2,1)S(1)}, u32[]{:S(2)}, u32[]{:S(2)}) async-start(bf16[32,16,768]{2,1,0:T(8,128)(2,1)} %pad_maximum_fusion), calls=%async_computation.2 | async-start | bytes 1572864 | tf_op jit(solution)/shard_map/all_to_all | solution.py:73
  95.5 39.3 %all-to-all-done.2 = bf16[32,16,768]{2,1,0:T(8,128)(2,1)S(1)} async-done(((bf16[32,16,768]{2,1,0:T(8,128)(2,1)}), bf16[32,16,768]{2,1,0:T(8,128)(2,1)S(1)}, u32[]{:S(2)}, u32[]{:S(2)}) %all-to-all-start.2) | async-done | bytes 786464 | tf_op jit(solution)/shard_map/all_to_all | solution.py:73
  134.9 0.2 copy.190
  135.1 0.1 copy.191
  135.6 0.5 fusion.8
  136.1 0.5 fusion.19
  136.7 0.3 copy.153
  137.1 0.3 convert_element_type.79
  137.4 29.6 %all_to_all.30 = bf16[32,16,384]{2,1,0:T(8,128)(2,1)S(1)} all-to-all(bf16[32,16,384]{2,1,0:T(8,128)(2,1)S(1)} %convert_element_type.79), channel_id=1, replica_groups=mesh['lat'=32,'lon'=16] {'lat'}, dimensions={0} | all-to-all | bytes 786432 | tf_op jit(solution)/shard_map/all_to_all | solution.py:111
  167.1 0.2 broadcast_in_dim.65
  167.4 50.4 %all_to_all.31 = bf16[16,2,48,256]{3,2,1,0:T(8,128)(2,1)S(1)} all-to-all(bf16[16,2,48,256]{3,2,1,0:T(8,128)(2,1)S(1)} %bitcast.236), channel_id=1, replica_groups=mesh['lat'=32,'lon'=16] {'lon'}, dimensions={0} | all-to-all | bytes 1572864 | tf_op jit(solution)/shard_map/all_to_all | solution.py:119
  217.9 0.7 convolution_convert_fusion.1
  218.7 0.6 copy.156
  219.5 15.2 %all_to_all.32 = bf16[8,180,256]{2,1,0:T(8,128)(2,1)S(1)} all-to-all(bf16[8,180,256]{2,1,0:T(8,128)(2,1)S(1)} %copy.158), channel_id=1, replica_groups={{0,1,4,5,8,9,12,13},{2,3,6,7,10,11,14,15},{16,17,20,21,24,25,28,29},{18..., dimensions={0} | all-to-all | bytes 1474560 | tf_op jit(solution)/shard_map/all_to_all | solution.py:124
  234.9 0.4 fusion.26
  235.3 0.7 copy-done.1
  236.0 0.5 add_convert_fusion
  236.5 1.3 copy.160
  (77 shorter events, 4.3 us)
Async XLA Ops:
  0.0 234.9 %copy-start = (bf16[256,256]{1,0:T(8,128)(2,1)S(1)}, bf16[256,256]{1,0:T(8,128)(2,1)}, u32[]{:S(2)}) copy-start(bf16[256,256]{1,0:T(8,128)(2,1)} %param.6) | copy-start | bytes 393220
  1.4 5.5 %copy-start.2 = (bf16[16,24,192]{2,1,0:T(8,128)(2,1)S(1)}, bf16[16,24,192]{2,1,0:T(8,128)(2,1)}, u32[]{:S(2)}) copy-start(bf16[16,24,192]{2,1,0:T(8,128)(2,1)} %param.5) | copy-start | bytes 442372
  2.4 17.2 %all-to-all-start = ((bf16[8,180,256]{2,1,0:T(8,128)(2,1)}), bf16[8,180,256]{2,1,0:T(8,128)(2,1)S(1)}, u32[]{:S(2)}, u32[]{:S(2)}) async-start(bf16[8,180,256]{2,1,0:T(8,128)(2,1)} %reshape.249), calls=%async_computation | async-start | bytes 1507328 | tf_op jit(solution)/shard_map/all_to_all | solution.py:52
  22.2 63.2 %all-to-all-start.1 = ((bf16[16,48,2,256]{3,1,2,0:T(8,128)(2,1)}), bf16[16,48,2,256]{3,1,2,0:T(8,128)(2,1)S(1)}, u32[]{:S(2)}, u32[]{:S(2)}) async-start(bf16[16,48,2,256]{3,1,2,0:T(8,128)(2,1)} %copy.119), calls=%async_computation.1 | async-start | bytes 1572864 | tf_op jit(solution)/shard_map/all_to_all | solution.py:57
  87.2 47.6 %all-to-all-start.2 = ((bf16[32,16,768]{2,1,0:T(8,128)(2,1)}), bf16[32,16,768]{2,1,0:T(8,128)(2,1)S(1)}, u32[]{:S(2)}, u32[]{:S(2)}) async-start(bf16[32,16,768]{2,1,0:T(8,128)(2,1)} %pad_maximum_fusion), calls=%async_computation.2 | async-start | bytes 1572864 | tf_op jit(solution)/shard_map/all_to_all | solution.py:73
  234.9 1.1 copy-start.1
  234.9 1.1 copy-start.3

commit v10 on v8

--- a/solution.py
+++ b/solution.py
@@ -115,8 +115,9 @@
         by_pair, (lon_count // 4, halves, 2, pair_rows, 2 * wave_dev, width)
     ).reshape(lon_count, pair_rows, 2 * wave_dev, width)
     pair_coeffs = lax.all_to_all(pair_send, "lon", 0, 0, tiled=True)
-    pair_coeffs = pair_coeffs.transpose(1, 0, 2, 3).reshape(pair_rows, 2 * wave_dev * lon_count, width)
-    half_grid = table_dot(table, pair_coeffs, (((1,), (1,)), ((), ())))
+    half_grid = table_dot(
+        table.reshape(group * lon_dev, lon_count, 2 * wave_dev), pair_coeffs, (((1, 2), (0, 2)), ((), ()))
+    )
     half_send = half_grid.astype(jnp.bfloat16).reshape(group, lon_dev, pair_rows, width).transpose(0, 2, 1, 3)
     half_send = half_send.reshape(group, pair_rows * lon_dev, width)
     spatial = lax.all_to_all(

time: 238 us -> 240 us (level)
  blocking collectives: 95.3 us -> 44.8 us
  waiting for transfers between devices: 86.9 us -> 134 us
  starting transfers between devices: 27.7 us -> 31.5 us
    all_to_all x1 -> x0, blocking collectives: 50.5 us -> none  [shards(): pair_coeffs = lax.all_to_all(pair_send, 'lon', 0, 0, tiled=True)]
    all_to_all x0 -> x1, waiting for transfers between devices: none -> 46.8 us  [shards(): pair_coeffs = lax.all_to_all(pair_send, 'lon', 0, 0, tiled=True)]
    all_to_all x0 -> x1, starting transfers between devices: none -> 3.79 us  [shards(): pair_coeffs = lax.all_to_all(pair_send, 'lon', 0, 0, tiled=True)]
  transfers between devices with their start and end apart: 3 -> 4, of which waited for: 3 -> 4; matrix products, arithmetic and copies ran while one was open for 5% -> 6% of each run, Pallas kernels for 0% -> 0%
where the time goes in v10:
time: 240 us; the launch traced here: 239 us
  waiting for transfers between devices  134 us (56%)
  blocking collectives  44.8 us (19%)
  starting transfers between devices  31.5 us (13%)
  local copies, waits for them, and re-layouts  14.2 us (6%)
  other arithmetic  10.6 us (4%)
  matrix products  3.58 us (1%)
    all_to_all x1, waiting for transfers between devices, shards(): pair_coeffs = lax.all_to_all(pair_send, 'lon', 0, 0, tiled=True)  46.8 us
    all_to_all x1, waiting for transfers between devices, shards(): lax.all_to_all(partial.astype(jnp.bfloat16).reshape(lon_count, 2 * wave_d...  44.8 us
    all_to_all x1, waiting for transfers between devices, shards(): lax.all_to_all(payload, 'lat', 0, 0, tiled=True).reshape(all_rows, -1)  39.3 us
    all_to_all x1, blocking collectives, shards(): lax.all_to_all(grad_units.reshape(lat_count, lat_rows, units_per_dev * un...  29.6 us
    all_to_all x1, blocking collectives, shards(): lax.all_to_all(half_send, 'lon', 0, 0, tiled=True, axis_index_groups=half...  15.2 us
    all_to_all x1, starting transfers between devices, shards(): lax.all_to_all(partial.astype(jnp.bfloat16).reshape(lon_count, 2 * wave_d...  14.9 us
    convert_element_type x1, other arithmetic, fourier_table(): return lax.optimization_barrier(table.astype(jnp.bfloat16))  9.23 us
    all_to_all x1, starting transfers between devices, shards(): lax.all_to_all(payload, 'lat', 0, 0, tiled=True).reshape(all_rows, -1)  8.2 us
  transfers between devices with their start and end apart: 4, of which 4 were waited for; matrix products, arithmetic and copies ran while one was open for 6% of the time, Pallas kernels for 0%

profile of v10, /device:TPU:32, one launch (start us, length us, event | category | flops | bytes accessed | tf_op | source)
XLA Modules:
  0.0 239.1 jit_solution(12433434843499675089)
XLA Ops:
  0.0 1.4 copy.371
  1.4 1.0 reshape.241
  2.4 4.6 %all-to-all-start = ((bf16[8,180,256]{2,1,0:T(8,128)(2,1)}), bf16[8,180,256]{2,1,0:T(8,128)(2,1)S(1)}, u32[]{:S(2)}, u32[]{:S(2)}) async-start(bf16[8,180,256]{2,1,0:T(8,128)(2,1)} %reshape.241), calls=%async_computation | async-start | bytes 1507328 | tf_op jit(solution)/shard_map/all_to_all | solution.py:52
  7.1 9.2 %fusion.4 = bf16[720,768]{1,0:T(8,128)(2,1)S(1)} fusion(s32[768]{0:T(1024)S(1)} %get-tuple-element.72, s32[768]{0:T(1024)S(1)} %get-tuple-element.73, s32[768]{0:T(1024)S(1)} %get-tuple-element.71, s32[768]{0:T(1024)S(1)} %get-tuple-element.74, s32[720]{0:T(1024)S(1)} %fusion.74, pred[768]{0:T(1024)(128)(4,1)S(1)} %get-tuple-element.75, ...), kind=kLoop, calls=%fused_computation.5 | loop fusion | flops 8294400 | bytes 1122624 | tf_op jit(solution)/shard_map/convert_element_type | solution.py:16
  16.3 0.3 fusion.89
  16.9 2.9 %all-to-all-done = bf16[8,180,256]{2,1,0:T(8,128)(2,1)S(1)} async-done(((bf16[8,180,256]{2,1,0:T(8,128)(2,1)}), bf16[8,180,256]{2,1,0:T(8,128)(2,1)S(1)}, u32[]{:S(2)}, u32[]{:S(2)}) %all-to-all-start) | async-done | bytes 737312 | tf_op jit(solution)/shard_map/all_to_all | solution.py:52
  19.9 0.6 copy.373
  20.5 0.8 convolution_convert_fusion
  21.3 1.0 copy.375
  22.3 14.9 %all-to-all-start.1 = ((bf16[16,48,2,256]{3,1,2,0:T(8,128)(2,1)}), bf16[16,48,2,256]{3,1,2,0:T(8,128)(2,1)S(1)}, u32[]{:S(2)}, u32[]{:S(2)}) async-start(bf16[16,48,2,256]{3,1,2,0:T(8,128)(2,1)} %copy.375), calls=%async_computation.1 | async-start | bytes 1572864 | tf_op jit(solution)/shard_map/all_to_all | solution.py:57
  38.8 1.3 stack.131
  40.1 44.8 %all-to-all-done.1 = bf16[16,48,2,256]{3,1,2,0:T(8,128)(2,1)S(1)} async-done(((bf16[16,48,2,256]{3,1,2,0:T(8,128)(2,1)}), bf16[16,48,2,256]{3,1,2,0:T(8,128)(2,1)S(1)}, u32[]{:S(2)}, u32[]{:S(2)}) %all-to-all-start.1) | async-done | bytes 786464 | tf_op jit(solution)/shard_map/all_to_all | solution.py:57
  84.9 0.2 reduce_sum.12
  85.5 1.3 copy.434
  86.8 8.2 %all-to-all-start.2 = ((bf16[32,16,768]{2,1,0:T(8,128)(2,1)}), bf16[32,16,768]{2,1,0:T(8,128)(2,1)S(1)}, u32[]{:S(2)}, u32[]{:S(2)}) async-start(bf16[32,16,768]{2,1,0:T(8,128)(2,1)} %copy.434), calls=%async_computation.2 | async-start | bytes 1572864 | tf_op jit(solution)/shard_map/all_to_all | solution.py:71
  95.1 39.3 %all-to-all-done.2 = bf16[32,16,768]{2,1,0:T(8,128)(2,1)S(1)} async-done(((bf16[32,16,768]{2,1,0:T(8,128)(2,1)}), bf16[32,16,768]{2,1,0:T(8,128)(2,1)S(1)}, u32[]{:S(2)}, u32[]{:S(2)}) %all-to-all-start.2) | async-done | bytes 786464 | tf_op jit(solution)/shard_map/all_to_all | solution.py:71
  135.2 0.5 fusion.8
  135.8 0.5 fusion.18
  136.3 0.3 copy.440
  136.7 0.3 convert_element_type.79
  137.0 29.6 %all_to_all.30 = bf16[32,16,384]{2,1,0:T(8,128)(2,1)S(1)} all-to-all(bf16[32,16,384]{2,1,0:T(8,128)(2,1)S(1)} %convert_element_type.79), channel_id=1, replica_groups=mesh['lat'=32,'lon'=16] {'lat'}, dimensions={0} | all-to-all | bytes 786432 | tf_op jit(solution)/shard_map/all_to_all | solution.py:109
  166.9 1.0 broadcast_in_dim.66
  167.9 3.8 %all-to-all-start.4 = ((bf16[16,2,48,256]{3,2,1,0:T(8,128)(2,1)}), bf16[16,2,48,256]{3,2,1,0:T(8,128)(2,1)S(1)}, u32[]{:S(2)}, u32[]{:S(2)}) async-start(bf16[16,2,48,256]{3,2,1,0:T(8,128)(2,1)} %bitcast.75), calls=%async_computation.4 | async-start | bytes 1572864 | tf_op jit(solution)/shard_map/all_to_all | solution.py:117
  171.7 0.6 copy.370
  172.3 46.8 %all-to-all-done.4 = bf16[16,2,48,256]{3,2,1,0:T(8,128)(2,1)S(1)} async-done(((bf16[16,2,48,256]{3,2,1,0:T(8,128)(2,1)}), bf16[16,2,48,256]{3,2,1,0:T(8,128)(2,1)S(1)}, u32[]{:S(2)}, u32[]{:S(2)}) %all-to-all-start.4) | async-done | bytes 786464 | tf_op jit(solution)/shard_map/all_to_all | solution.py:117
  219.2 0.8 bitcast_convert_fusion
  219.9 0.6 copy.443
  220.8 15.2 %all_to_all.31 = bf16[8,180,256]{2,1,0:T(8,128)(2,1)S(1)} all-to-all(bf16[8,180,256]{2,1,0:T(8,128)(2,1)S(1)} %copy.445), channel_id=1, replica_groups={{0,1,4,5,8,9,12,13},{2,3,6,7,10,11,14,15},{16,17,20,21,24,25,28,29},{18..., dimensions={0} | all-to-all | bytes 1474560 | tf_op jit(solution)/shard_map/all_to_all | solution.py:123
  236.2 0.4 fusion.25
  236.6 0.7 copy-done.1
  237.3 0.5 add_convert_fusion
  237.8 1.3 copy.447
  (85 shorter events, 3.6 us)
Async XLA Ops:
  0.0 236.1 %copy-start = (bf16[256,256]{1,0:T(8,128)(2,1)S(1)}, bf16[256,256]{1,0:T(8,128)(2,1)}, u32[]{:S(2)}) copy-start(bf16[256,256]{1,0:T(8,128)(2,1)} %param.6) | copy-start | bytes 393220
  2.4 13.9 %copy-start.2 = (bf16[16,24,192]{2,1,0:T(8,128)(2,1)S(1)}, bf16[16,24,192]{2,1,0:T(8,128)(2,1)}, u32[]{:S(2)}) copy-start(bf16[16,24,192]{2,1,0:T(8,128)(2,1)} %param.5) | copy-start | bytes 442372
  2.4 17.4 %all-to-all-start = ((bf16[8,180,256]{2,1,0:T(8,128)(2,1)}), bf16[8,180,256]{2,1,0:T(8,128)(2,1)S(1)}, u32[]{:S(2)}, u32[]{:S(2)}) async-start(bf16[8,180,256]{2,1,0:T(8,128)(2,1)} %reshape.241), calls=%async_computation | async-start | bytes 1507328 | tf_op jit(solution)/shard_map/all_to_all | solution.py:52
  22.3 62.6 %all-to-all-start.1 = ((bf16[16,48,2,256]{3,1,2,0:T(8,128)(2,1)}), bf16[16,48,2,256]{3,1,2,0:T(8,128)(2,1)S(1)}, u32[]{:S(2)}, u32[]{:S(2)}) async-start(bf16[16,48,2,256]{3,1,2,0:T(8,128)(2,1)} %copy.375), calls=%async_computation.1 | async-start | bytes 1572864 | tf_op jit(solution)/shard_map/all_to_all | solution.py:57
  86.8 47.6 %all-to-all-start.2 = ((bf16[32,16,768]{2,1,0:T(8,128)(2,1)}), bf16[32,16,768]{2,1,0:T(8,128)(2,1)S(1)}, u32[]{:S(2)}, u32[]{:S(2)}) async-start(bf16[32,16,768]{2,1,0:T(8,128)(2,1)} %copy.434), calls=%async_computation.2 | async-start | bytes 1572864 | tf_op jit(solution)/shard_map/all_to_all | solution.py:71
  167.9 51.3 %all-to-all-start.4 = ((bf16[16,2,48,256]{3,2,1,0:T(8,128)(2,1)}), bf16[16,2,48,256]{3,2,1,0:T(8,128)(2,1)S(1)}, u32[]{:S(2)}, u32[]{:S(2)}) async-start(bf16[16,2,48,256]{3,2,1,0:T(8,128)(2,1)} %bitcast.75), calls=%async_computation.4 | async-start | bytes 1572864 | tf_op jit(solution)/shard_map/all_to_all | solution.py:117
  236.1 1.1 copy-start.1
  236.2 1.1 copy-start.3
